TPU v7x, 256 devices: a whole 4x4x8 slice. The times are simulated.
256 devices in a mesh: tile: 64 (over y_hi, z, x), fsdp: 4 (over y_lo, core).
Axes of the slice: x: 4, y: 4 (y_hi: 2, y_lo: 2; y = y_hi * 2 + y_lo), z: 8, core: 2. Of those that a mesh axis runs over, the one named last changes fastest.
Arguments:
- fields: bfloat16 [4, 32, 512, 512], P('fsdp', None, 'tile'), may hold values from -6 to 6
- seam_shift: int32 [64, 2], P('tile'), may hold values from -4 to 4
- kernel: float32 [49, 512], replicated, may hold values from -0.875 to 0.875
- gain: float32 [512], replicated, may hold values from 0.3 to 3
- w_in: bfloat16 [512, 2048], P(None, 'fsdp'), may hold values from -0.25 to 0.25
- w_out: bfloat16 [2048, 512], P('fsdp'), may hold values from -0.125 to 0.125
- cotangent: bfloat16 [4, 32, 512, 512], P('fsdp', None, 'tile'), may hold values from -6 to 6
Outputs:
- mixed: bfloat16 [4, 32, 512, 512], P('fsdp', None, 'tile')
- field_grad: bfloat16 [4, 32, 512, 512], P('fsdp', None, 'tile')
- kernel_grad: float32 [49, 512], replicated
- gain_grad: float32 [512], replicated
- w_in_grad: float32 [512, 2048], P(None, 'fsdp')
- w_out_grad: float32 [2048, 512], P('fsdp')
Inputs may be any that keep to these rules, and one draw needn't show every extreme that they name: `seam_shift`: offset added to the row index of cells taken across a tile's west (column 0) or east (column 1) seam.
All inputs are finite; a program needn't handle non-finite values.
Results may differ from a plain program's by a relative error of at most 0.0095.
Values may be sent and summed in bfloat16 or wider, within the bound.
No kernel may reach another device: no remote copies, remote signals or barrier semaphores. Data moves between devices by JAX's collectives and lax.ppermute only.
A program may use at most 128 MiB of HBM per device.

v0:
```python
import math

import jax
import jax.numpy as jnp
from jax import lax
from jax.sharding import PartitionSpec as P

eps = 1e-06
inv_root2 = 0.7071067811865476
inv_root_tau = 0.3989422804014327


def extended(cells, sides, width):
    for axis, dim in sides:
        count = lax.axis_size(axis)
        head = lax.slice_in_dim(cells, 0, width, axis=dim)
        tail = lax.slice_in_dim(cells, cells.shape[dim] - width, cells.shape[dim], axis=dim)
        cells = jnp.concatenate(
            [
                lax.ppermute(tail, axis, [(i, (i + 1) % count) for i in range(count)]),
                cells,
                lax.ppermute(head, axis, [((i + 1) % count, i) for i in range(count)]),
            ],
            axis=dim,
        )
    return cells


def exchange(value, axis, bit):
    count = lax.axis_size(axis)
    return lax.ppermute(value, axis, [(i, i ^ (1 << bit)) for i in range(count)])


def fsdp_summed(stacked):
    me = lax.axis_index("fsdp")
    for bit in (0, 1):
        half = stacked.shape[0] // 2
        side = (me >> bit) & 1
        keep = lax.dynamic_slice_in_dim(stacked, side * half, half, 0).astype(jnp.bfloat16)
        send = lax.dynamic_slice_in_dim(stacked, (1 - side) * half, half, 0).astype(jnp.bfloat16)
        got = exchange(send, "fsdp", bit)
        stacked = keep.astype(jnp.float32) + got.astype(jnp.float32)
    return stacked


def tile_summed(chunk):
    assert lax.axis_size("tile") == 64
    me = lax.axis_index("tile")
    groups = ((0, 1), (2, 3), (4, 5))

    def masks(group):
        mine = ((me >> group[0]) & 1) * 2 + ((me >> group[1]) & 1)
        return mine, [(d, ((d >> 1) << group[0]) | ((d & 1) << group[1])) for d in (1, 2, 3)]

    for group in groups:
        mine, partners = masks(group)
        size = chunk.shape[0] // 4
        total = lax.dynamic_slice_in_dim(chunk, mine * size, size, 0)
        for d, mask in partners:
            send = lax.dynamic_slice_in_dim(chunk, (mine ^ d) * size, size, 0)
            total = total + swapped(send.astype(jnp.bfloat16), "tile", mask).astype(jnp.float32)
        chunk = total
    chunk = chunk.astype(jnp.bfloat16)
    for group in reversed(groups):
        mine, partners = masks(group)
        size = chunk.shape[0]
        whole = jnp.zeros((4 * size,) + chunk.shape[1:], chunk.dtype)
        whole = lax.dynamic_update_slice_in_dim(whole, chunk, mine * size, 0)
        for d, mask in partners:
            got = swapped(chunk, "tile", mask)
            whole = lax.dynamic_update_slice_in_dim(whole, got, (mine ^ d) * size, 0)
        chunk = whole
    return chunk.astype(jnp.float32)


def swapped(value, axis, mask):
    count = lax.axis_size(axis)
    return lax.ppermute(value, axis, [(i, i ^ mask) for i in range(count)])


def gathered_rows(shard):
    me = lax.axis_index("fsdp")
    for bit in (0, 1):
        side = (me >> bit) & 1
        got = exchange(shard, "fsdp", bit)
        shard = jnp.concatenate(
            [jnp.where(side == 0, shard, got), jnp.where(side == 0, got, shard)], axis=0
        )
    return shard


def gelu(value):
    return value * 0.5 * (1.0 + lax.erf(value * inv_root2))


def gelu_slope(value):
    return 0.5 * (1.0 + lax.erf(value * inv_root2)) + value * inv_root_tau * jnp.exp(
        -0.5 * value * value
    )


def shift_rows(strip, offset):
    height = strip.shape[1]
    wider = jnp.pad(strip, ((0, 0), (height, height), (0, 0), (0, 0)))
    return lax.dynamic_slice_in_dim(wider, height + offset, height, 1)


def depthwise(padded, kernel):
    height = padded.shape[1] - 6
    width = padded.shape[2] - 6
    total = jnp.zeros((padded.shape[0], height, width, padded.shape[3]), jnp.float32)
    for row in range(7):
        for col in range(7):
            total = (
                total + padded[:, row : row + height, col : col + width, :] * kernel[7 * row + col]
            )
    return total


def body(fields, seam_shift, kernel, gain, w_in, w_out, cotangent):
    height = fields.shape[1]
    width = fields.shape[2]
    channels = fields.shape[3]
    count = fields.shape[0] * height * width
    cells = count * lax.axis_size("tile") * lax.axis_size("fsdp")
    factor = 1.0 / math.sqrt(cells)
    west_shift = seam_shift[0, 0]
    east_shift = seam_shift[0, 1]
    row_pad = ((0, 0), (3, 3), (0, 0), (0, 0))
    widened = extended(fields, (("tile", 2),), 3)
    west = shift_rows(widened[:, :, :3], west_shift)
    east = shift_rows(widened[:, :, width + 3 :], east_shift)
    padded = jnp.pad(jnp.concatenate([west, fields, east], axis=2), row_pad)
    mixed_in = depthwise(padded, kernel)
    rows = mixed_in.reshape(count, channels)
    mean = jnp.mean(rows, axis=-1, keepdims=True)
    centered = rows - mean
    rstd = lax.rsqrt(jnp.mean(centered * centered, axis=-1, keepdims=True) + eps)
    normed = centered * rstd
    scaled = (normed * gain).astype(jnp.bfloat16)
    back = cotangent.reshape(count, channels)
    contract_last = (((1,), (1,)), ((), ()))
    full_in, full_out = (
        lax.all_gather(w_in, "fsdp", axis=1, tiled=True),
        gathered_rows(w_out),
    )
    pre = jnp.dot(scaled, full_in, preferred_element_type=jnp.float32)
    hidden = gelu(pre).astype(jnp.bfloat16)
    branch = jnp.dot(hidden, full_out, preferred_element_type=jnp.float32)
    d_hidden = lax.dot_general(back, full_out, contract_last, preferred_element_type=jnp.float32)
    residual = fields.reshape(count, channels).astype(jnp.float32)
    mixed = (residual + branch).astype(jnp.bfloat16).reshape(fields.shape)
    d_pre = (d_hidden * gelu_slope(pre)).astype(jnp.bfloat16)
    d_scaled = lax.dot_general(d_pre, full_in, contract_last, preferred_element_type=jnp.float32)
    term_gain = jnp.sum(d_scaled * normed, axis=0) * factor
    d_normed = d_scaled * gain
    d_rows = (
        d_normed
        - jnp.mean(d_normed, axis=-1, keepdims=True)
        - normed * jnp.mean(d_normed * normed, axis=-1, keepdims=True)
    ) * rstd
    d_mixed = d_rows.reshape(mixed_in.shape)
    unused, pullback = jax.vjp(depthwise, padded.astype(jnp.float32), kernel)
    d_padded, kernel_term = pullback(d_mixed)
    kernel_term = kernel_term * factor
    d_core = d_padded[:, 3 : height + 3]
    d_west = shift_rows(d_core[:, :, :3], -west_shift)
    d_east = shift_rows(d_core[:, :, width + 3 :], -east_shift)
    returned = extended(
        jnp.concatenate([d_west, d_east], axis=2).astype(jnp.bfloat16), (("tile", 2),), 3
    ).astype(jnp.float32)
    own = cotangent.astype(jnp.float32) + d_core[:, :, 3 : width + 3]
    field_grad = jnp.concatenate(
        [
            own[:, :, :3] + returned[:, :, :3],
            own[:, :, 3 : width - 3],
            own[:, :, width - 3 :] + returned[:, :, 9:],
        ],
        axis=2,
    ).astype(jnp.bfloat16)
    parts = lax.axis_size("fsdp")
    assert parts == 4
    share = full_in.shape[1] // parts
    d_pre4 = d_pre.reshape(count, 2, 2, share)
    hidden4 = hidden.reshape(count, 2, 2, share)
    term_in4 = jnp.einsum("ck,cabh->bakh", scaled, d_pre4, preferred_element_type=jnp.float32)
    term_out4 = jnp.einsum("cabh,cj->bahj", hidden4, back, preferred_element_type=jnp.float32)
    spare = -(kernel_term.shape[0] + 1) % 64
    small = jnp.concatenate(
        [kernel_term, term_gain[None], jnp.zeros((spare, channels), jnp.float32)], axis=0
    )
    small4 = jnp.broadcast_to(small, (2, 2) + small.shape)
    stacked = jnp.concatenate(
        [
            (term_in4 * factor).astype(jnp.bfloat16),
            small4.astype(jnp.bfloat16),
            (term_out4 * factor).astype(jnp.bfloat16),
        ],
        axis=2,
    ).reshape(-1, channels)
    chunk = fsdp_summed(stacked)
    first = channels + small.shape[0]
    total = tile_summed(chunk)
    low, high = total[:first], total[first:]
    w_in_grad = low[:channels]
    kernel_grad = low[channels : channels + kernel_term.shape[0]]
    gain_grad = low[channels + kernel_term.shape[0]]
    w_out_grad = high
    return (mixed, field_grad, kernel_grad, gain_grad, w_in_grad, w_out_grad)


def solution(mesh):
    return jax.shard_map(
        body,
        mesh=mesh,
        in_specs=(
            P("fsdp", None, "tile", None),
            P("tile", None),
            P(),
            P(),
            P(None, "fsdp"),
            P("fsdp", None),
            P("fsdp", None, "tile", None),
        ),
        out_specs=(
            P("fsdp", None, "tile", None),
            P("fsdp", None, "tile", None),
            P(),
            P(),
            P(None, "fsdp"),
            P("fsdp", None),
        ),
        check_vma=False,
    )
```

profile of v0, /device:TPU:32, one launch (start us, length us, event | category | flops | bytes accessed | tf_op | source)
XLA Modules:
  0.0 221.3 jit_solution(6539928569547449269)
XLA Ops:
  7.2 0.7 all-gather.2.cloned.1.call-update
  7.9 1.1 fusion.120
  9.1 1.6 collective-permute-start
  10.6 2.6 %collective-permute-start.1 = (bf16[1,32,3,512]{3,2,1,0:T(4,128)(2,1)S(1)}, bf16[1,32,3,512]{3,2,1,0:T(4,128)(2,1)S(1)}, u32[]{:S(2)}, u32[]{:S(2)}) collective-permute-start(bf16[1,32,3,512]{3,2,1,0:T(4,128)(2,1)S(1)} %get-tuple-element.129), channel_id=1, source_target_pairs={{4,0},{8,4},{12,8},{16,12},{20,16},{24,20},{28,24},{32,28},{36,32}... | collective-permute-start | bytes 294920 | tf_op jit(solution)/shard_map/ppermute | solution.py:22
  13.3 1.1 fusion.121
  14.4 1.1 fusion.122
  15.6 1.0 fusion.123
  20.7 0.7 copy-done.10
  21.5 1.0 pad_maximum_fusion.10
  22.5 1.6 collective-permute-start.3
  24.1 4.6 %fusion.116 = (f32[32,8]{1,0:T(8,128)S(1)}, f32[1,32,8,512]{3,2,1,0:T(8,128)S(1)}) fusion(f32[512]{0:T(512)S(1)} %bitcast.304, bf16[1,38,14,512]{3,2,1,0:T(8,128)(2,1)S(1)} %get-tuple-element.60, f32[512]{0:T(512)S(1)} %bitcast.340, f32[512]{0:T(512)S(1)} %bitcast.342, f32[512]{0:T(512)S(1)} %bitcast.344, f32[512]{0:T(512)S(1)} %bitcast.346, ...), kind=kLoop, calls=%fused_computation.288 | loop fusion | flops 21626624 | bytes 12094464 | tf_op jit(solution)/shard_map/reduce_sum | solution.py:136
  29.1 36.1 %collective-permute-done.3 = bf16[1024,512]{1,0:T(8,128)(2,1)} collective-permute-done((bf16[1024,512]{1,0:T(8,128)(2,1)}, bf16[1024,512]{1,0:T(8,128)(2,1)}, u32[]{:S(2)}, u32[]{:S(2)}) %collective-permute-start.3) | collective-permute-done | bytes 1048608 | tf_op jit(solution)/shard_map/ppermute | solution.py:31
  65.2 3.0 %broadcast_select_fusion.1 = (bf16[1024,512]{1,0:T(8,128)(2,1)}, bf16[1024,512]{1,0:T(8,128)(2,1)}) fusion(bf16[1024,512]{1,0:T(8,128)(2,1)} %collective-permute-done.3, pred[]{:T(512)S(6)} %eq.8, bf16[512,512]{1,0:T(8,128)(2,1)S(1)} %get-tuple-element.75, bf16[512,512]{1,0:T(8,128)(2,1)S(1)} %get-tuple-element.74), kind=kLoop, calls=%fused_computation.30 | loop fusion | flops 3145728 | bytes 4194305 | tf_op jit(solution)/shard_map/jit(_where)/select_n | solution.py:87
  68.2 2.6 %multiply_convert_fusion.2 = (bf16[256,2048]{1,0:T(8,128)(2,1)S(1)}, f32[256,2048]{1,0:T(8,128)S(1)}) fusion(bf16[512,2048]{1,0:T(8,128)(2,1)} %all-gather.2.cloned.1.call-done, f32[1,32,8,512]{3,2,1,0:T(8,128)S(1)} %get-tuple-element.62, f32[512]{0:T(512)S(1)} %copy-done.59, f32[256]{0:T(256)S(1)} %rsqrt.13, f32[256]{0:T(256)S(1)} %div.15), kind=kOutput, calls=%fused_computation.15 | convolution fusion | flops 540016640 | bytes 5771264 | tf_op jit(solution)/shard_map/dot_general | solution.py:147
  70.9 4.1 %fusion.1 = bf16[256,2048]{1,0:T(8,128)(2,1)} fusion(f32[256,2048]{1,0:T(8,128)S(1)} %get-tuple-element.185, bf16[1024,512]{1,0:T(8,128)(2,1)S(1)} %copy-done.5, bf16[1024,512]{1,0:T(8,128)(2,1)S(1)} %copy-done.3, bf16[1,32,8,512]{3,2,1,0:T(8,128)(2,1)S(1)} %copy-done.7), kind=kOutput, calls=%fused_computation.7 | convolution fusion | flops 546308096 | bytes 5505024 | tf_op jit(solution)/shard_map/dot_general | solution.py:150
  74.9 2.6 %reshape.1291 = bf16[256,2,2,512]{3,2,1,0:T(2,128)(2,1)} reshape(bf16[256,2048]{1,0:T(8,128)(2,1)} %fusion.1) | data formatting | bytes 2097152 | tf_op jit(solution)/shard_map/reshape | solution.py:184
  77.6 2.8 %multiply_reduce_fusion = (f32[512]{0:T(512)S(1)}, f32[256]{0:T(256)S(1)}, f32[256]{0:T(256)S(1)}, f32[256,512]{1,0:T(8,128)S(1)}) fusion(f32[1,32,8,512]{3,2,1,0:T(8,128)S(1)} %get-tuple-element.62, f32[256]{0:T(256)S(1)} %rsqrt.13, f32[256]{0:T(256)S(1)} %div.15, f32[512]{0:T(512)S(1)} %copy-done.59, bf16[256,2048]{1,0:T(8,128)(2,1)} %fusion.1, ...), kind=kOutput, calls=%fused_computation.227 | convolution fusion | flops 537918464 | bytes 4202496 | tf_op jit(solution)/shard_map/dot_general | solution.py:154
  80.4 2.7 %fusion.89 = (f32[512]{0:T(512)}, f32[512]{0:T(512)}, f32[512]{0:T(512)}, f32[512]{0:T(512)}, f32[512]{0:T(512)}, /*index=5*/f32[512]{0:T(512)}, f32[512]{0:T(51...) fusion(f32[1,38,14,512]{3,2,1,0:T(8,128)S(1)} %get-tuple-elemen, ...), kind=kLoop, calls=%fused_computation.170 | loop fusion | flops 4318720 | bytes 8421376 | tf_op jit(solution)/shard_map/transpose(jvp())/reduce_sum | solution.py:115
  83.1 1.5 fusion.90
  84.6 1.6 fusion.91
  86.9 2.2 fusion.5
  89.4 0.7 fusion.6
  90.5 1.0 multiply_convert_fusion.6
  91.5 0.8 maximum_maximum_fusion
  93.0 1.7 constant_dynamic-slice_fusion
  94.7 1.0 copy-done
  97.2 0.9 bitcast_multiply_fusion.46
  98.2 1.3 bitcast_multiply_fusion.47
  99.5 1.3 bitcast_multiply_fusion.48
  100.8 2.3 %convert_add_fusion = bf16[2176,512]{1,0:T(8,128)(2,1)S(1)} fusion(bf16[2176,512]{1,0:T(8,128)(2,1)} %collective-permute-done.6, bf16[4352,512]{1,0:T(8,128)(2,1)S(1)} %bitcast.268, s32[]{:T(128)S(6)} %select_n.106), kind=kLoop, calls=%fused_computation.1 | loop fusion | flops 4456448 | bytes 6684676 | tf_op jit(solution)/shard_map/add | solution.py:42
  103.2 1.7 collective-permute-start.7
  104.9 6.7 %pad_add_fusion = f32[1,38,14,512]{3,2,1,0:T(8,128)S(1)} fusion(f32[1,32,8,512]{3,2,1,0:T(8,128)S(1)} %get-tuple-element.80, f32[1,32,8,512]{3,2,1,0:T(8,128)S(1)} %get-tuple-element.81, f32[1,32,8,512]{3,2,1,0:T(8,128)S(1)} %get-tuple-element.82, f32[1,32,8,512]{3,2,1,0:T(8,128)S(1)} %get-tuple-element.83, f32[1,32,8,512]{3,2,1,0:T(8,128)S(1)} %get-tuple-element.84, ...), kind=kLoop, calls=%fused_computation.22 | loop fusion | flops 13074432 | bytes 26779648 | tf_op jit(solution)/shard_map/transpose(jvp())/add_any | solution.py:115
  112.0 18.2 %collective-permute-done.7 = bf16[1088,512]{1,0:T(8,128)(2,1)S(1)} collective-permute-done((bf16[1088,512]{1,0:T(8,128)(2,1)S(1)}, bf16[1088,512]{1,0:T(8,128)(2,1)S(1)}, u32[]{:S(2)}, u32[]{:S(2)}) %collective-permute-start.7) | collective-permute-done | bytes 1114144 | tf_op jit(solution)/shard_map/ppermute | solution.py:31
  130.7 1.0 collective-permute-start.8
  131.7 1.1 collective-permute-start.10
  132.8 1.4 collective-permute-start.9
  134.3 1.4 fusion.11
  135.7 6.1 %collective-permute-done.8 = bf16[272,512]{1,0:T(8,128)(2,1)S(1)} collective-permute-done((bf16[272,512]{1,0:T(8,128)(2,1)S(1)}, bf16[272,512]{1,0:T(8,128)(2,1)S(1)}, u32[]{:S(2)}, u32[]{:S(2)}) %collective-permute-start.8) | collective-permute-done | bytes 278560 | tf_op jit(solution)/shard_map/ppermute | solution.py:78
  141.9 4.6 %collective-permute-done.10 = bf16[272,512]{1,0:T(8,128)(2,1)S(1)} collective-permute-done((bf16[272,512]{1,0:T(8,128)(2,1)S(1)}, bf16[272,512]{1,0:T(8,128)(2,1)S(1)}, u32[]{:S(2)}, u32[]{:S(2)}) %collective-permute-start.10) | collective-permute-done | bytes 278560 | tf_op jit(solution)/shard_map/ppermute | solution.py:78
  146.6 3.4 %collective-permute-start.11 = (bf16[68,512]{1,0:T(8,128)(2,1)S(1)}, bf16[68,512]{1,0:T(8,128)(2,1)S(1)}, u32[]{:S(2)}, u32[]{:S(2)}) collective-permute-start(bf16[68,512]{1,0:T(8,128)(2,1)S(1)} %get-tuple-element.76), channel_id=1, source_target_pairs={{0,32},{4,36},{8,40},{12,44},{16,48},{20,52},{24,56},{28,60},{32,0... | collective-permute-start | bytes 208904 | tf_op jit(solution)/shard_map/ppermute | solution.py:78
  150.0 1.6 collective-permute-start.12
  151.7 2.9 %collective-permute-done.11 = bf16[68,512]{1,0:T(8,128)(2,1)S(1)} collective-permute-done((bf16[68,512]{1,0:T(8,128)(2,1)S(1)}, bf16[68,512]{1,0:T(8,128)(2,1)S(1)}, u32[]{:S(2)}, u32[]{:S(2)}) %collective-permute-start.11) | collective-permute-done | bytes 69664 | tf_op jit(solution)/shard_map/ppermute | solution.py:78
  154.6 2.1 collective-permute-done.13
  156.8 2.9 %collective-permute-start.14 = (bf16[17,512]{1,0:T(8,128)(2,1)S(1)}, bf16[17,512]{1,0:T(8,128)(2,1)S(1)}, u32[]{:S(2)}, u32[]{:S(2)}) collective-permute-start(bf16[17,512]{1,0:T(8,128)(2,1)S(1)} %get-tuple-element.130), channel_id=1, source_target_pairs={{0,128},{4,132},{8,136},{12,140},{16,144},{20,148},{24,152},{28,15... | collective-permute-start | bytes 52232 | tf_op jit(solution)/shard_map/ppermute | solution.py:78
  159.8 6.1 %collective-permute-start.16 = (bf16[17,512]{1,0:T(8,128)(2,1)S(1)}, bf16[17,512]{1,0:T(8,128)(2,1)S(1)}, u32[]{:S(2)}, u32[]{:S(2)}) collective-permute-start(bf16[17,512]{1,0:T(8,128)(2,1)S(1)} %get-tuple-element.131), channel_id=1, source_target_pairs={{0,192},{4,196},{8,200},{12,204},{16,208},{20,212},{24,216},{28,22... | collective-permute-start | bytes 52232 | tf_op jit(solution)/shard_map/ppermute | solution.py:78
  166.3 3.6 %collective-permute-done.16 = bf16[17,512]{1,0:T(8,128)(2,1)S(1)} collective-permute-done((bf16[17,512]{1,0:T(8,128)(2,1)S(1)}, bf16[17,512]{1,0:T(8,128)(2,1)S(1)}, u32[]{:S(2)}, u32[]{:S(2)}) %collective-permute-start.16) | collective-permute-done | bytes 17440 | tf_op jit(solution)/shard_map/ppermute | solution.py:78
  169.9 4.0 %collective-permute-done.15 = bf16[17,512]{1,0:T(8,128)(2,1)S(1)} collective-permute-done((bf16[17,512]{1,0:T(8,128)(2,1)S(1)}, bf16[17,512]{1,0:T(8,128)(2,1)S(1)}, u32[]{:S(2)}, u32[]{:S(2)}) %collective-permute-start.15) | collective-permute-done | bytes 17440 | tf_op jit(solution)/shard_map/ppermute | solution.py:78
  173.9 3.0 %collective-permute-start.19 = (bf16[17,512]{1,0:T(8,128)(2,1)S(1)}, bf16[17,512]{1,0:T(8,128)(2,1)S(1)}, u32[]{:S(2)}, u32[]{:S(2)}) collective-permute-start(bf16[17,512]{1,0:T(8,128)(2,1)S(1)} %add_convert_fusion), channel_id=1, source_target_pairs={{0,192},{4,196},{8,200},{12,204},{16,208},{20,212},{24,216},{28,22... | collective-permute-start | bytes 52232 | tf_op jit(solution)/shard_map/ppermute | solution.py:78
  176.9 5.4 %collective-permute-start.18 = (bf16[17,512]{1,0:T(8,128)(2,1)S(1)}, bf16[17,512]{1,0:T(8,128)(2,1)S(1)}, u32[]{:S(2)}, u32[]{:S(2)}) collective-permute-start(bf16[17,512]{1,0:T(8,128)(2,1)S(1)} %add_convert_fusion), channel_id=1, source_target_pairs={{0,64},{4,68},{8,72},{12,76},{16,80},{20,84},{24,88},{28,92},{32,9... | collective-permute-start | bytes 52232 | tf_op jit(solution)/shard_map/ppermute | solution.py:78
  183.1 1.1 collective-permute-start.5
  184.1 1.0 collective-permute-start.4
  185.6 2.0 collective-permute-done.17
  188.9 2.1 collective-permute-start.21
  191.0 1.2 collective-permute-start.20
  193.0 3.2 %collective-permute-done.20 = bf16[68,512]{1,0:T(8,128)(2,1)S(1)} collective-permute-done((bf16[68,512]{1,0:T(8,128)(2,1)S(1)}, bf16[68,512]{1,0:T(8,128)(2,1)S(1)}, u32[]{:S(2)}, u32[]{:S(2)}) %collective-permute-start.20) | collective-permute-done | bytes 69664 | tf_op jit(solution)/shard_map/ppermute | solution.py:78
  196.6 0.7 dynamic_update_slice.42
  197.4 0.7 dynamic_update_slice.43
  198.1 1.6 collective-permute-start.23
  200.0 2.5 %collective-permute-start.24 = (bf16[272,512]{1,0:T(8,128)(2,1)S(1)}, bf16[272,512]{1,0:T(8,128)(2,1)S(1)}, u32[]{:S(2)}, u32[]{:S(2)}) collective-permute-start(bf16[272,512]{1,0:T(8,128)(2,1)S(1)} %dynamic_update_slice.43), channel_id=1, source_target_pairs={{0,4},{4,0},{8,12},{12,8},{16,20},{20,16},{24,28},{28,24},{32,36},... | collective-permute-start | bytes 835592 | tf_op jit(solution)/shard_map/ppermute | solution.py:78
  202.5 0.9 pad_maximum_fusion.13
  203.7 3.3 %collective-permute-done.23 = bf16[272,512]{1,0:T(8,128)(2,1)S(1)} collective-permute-done((bf16[272,512]{1,0:T(8,128)(2,1)S(1)}, bf16[272,512]{1,0:T(8,128)(2,1)S(1)}, u32[]{:S(2)}, u32[]{:S(2)}) %collective-permute-start.23) | collective-permute-done | bytes 278560 | tf_op jit(solution)/shard_map/ppermute | solution.py:78
  207.0 2.6 %collective-permute-done.24 = bf16[272,512]{1,0:T(8,128)(2,1)S(1)} collective-permute-done((bf16[272,512]{1,0:T(8,128)(2,1)S(1)}, bf16[272,512]{1,0:T(8,128)(2,1)S(1)}, u32[]{:S(2)}, u32[]{:S(2)}) %collective-permute-start.24) | collective-permute-done | bytes 278560 | tf_op jit(solution)/shard_map/ppermute | solution.py:78
  209.6 1.5 collective-permute-done.25
  212.4 1.6 fusion.119
  (208 shorter events, 11.4 us)
Async XLA Ops:
  7.2 13.2 %copy-start.1 = (bf16[1,32,8,512]{3,2,1,0:T(8,128)(2,1)S(1)}, bf16[1,32,8,512]{3,2,1,0:T(8,128)(2,1)}, u32[]{:S(2)}) copy-start(bf16[1,32,8,512]{3,2,1,0:T(8,128)(2,1)} %param.7) | copy-start | bytes 786436
  7.2 9.4 %copy-start.65 = (s32[1,2]{1,0:T(1,128)S(1)}, s32[1,2]{1,0:T(1,128)}, u32[]{:S(2)}) copy-start(s32[1,2]{1,0:T(1,128)} %param.8) | copy-start | bytes 28
  7.2 61.0 %all-gather.2.cloned.1.call-start = ((), (), s32[]{:S(2)}) async-start(), calls=%async_computation | async-start | bytes 2621440 | tf_op jit(solution)/shard_map/all_gather | solution.py:144
  9.1 11.0 %collective-permute-start = (bf16[1,32,3,512]{3,2,1,0:T(4,128)(2,1)S(1)}, bf16[1,32,3,512]{3,2,1,0:T(4,128)(2,1)S(1)}, u32[]{:S(2)}, u32[]{:S(2)}) collective-permute-start(bf16[1,32,3,512]{3,2,1,0:T(4,128)(2,1)S(1)} %get-tuple-element.128), channel_id=1, source_target_pairs={{0,4},{4,8},{8,12},{12,16},{16,20},{20,24},{24,28},{28,32},{32,36}... | collective-permute-start | bytes 294920 | tf_op jit(solution)/shard_map/ppermute | solution.py:20
  10.6 9.6 %collective-permute-start.1 = (bf16[1,32,3,512]{3,2,1,0:T(4,128)(2,1)S(1)}, bf16[1,32,3,512]{3,2,1,0:T(4,128)(2,1)S(1)}, u32[]{:S(2)}, u32[]{:S(2)}) collective-permute-start(bf16[1,32,3,512]{3,2,1,0:T(4,128)(2,1)S(1)} %get-tuple-element.129), channel_id=1, source_target_pairs={{4,0},{8,4},{12,8},{16,12},{20,16},{24,20},{28,24},{32,28},{36,32}... | collective-permute-start | bytes 294920 | tf_op jit(solution)/shard_map/ppermute | solution.py:22
  13.3 7.4 %collective-permute-start.2 = (bf16[512,512]{1,0:T(8,128)(2,1)}, bf16[512,512]{1,0:T(8,128)(2,1)S(1)}, u32[]{:S(2)}, u32[]{:S(2)}) collective-permute-start(bf16[512,512]{1,0:T(8,128)(2,1)} %param.12), channel_id=1, source_target_pairs={{0,1},{1,0},{2,3},{3,2},{4,5},{5,4},{6,7},{7,6},{8,9},{9,8},{10,11... | collective-permute-start | bytes 1572872 | tf_op jit(solution)/shard_map/ppermute | solution.py:31
  14.4 9.7 %copy-start.11 = (f32[1,512]{1,0:T(1,128)}, f32[1,512]{1,0:T(1,128)S(1)}, u32[]{:S(2)}) copy-start(f32[1,512]{1,0:T(1,128)S(1)} %get-tuple-element.142) | copy-start | bytes 6148
  14.4 9.7 %copy-start.13 = (f32[1,512]{1,0:T(1,128)}, f32[1,512]{1,0:T(1,128)S(1)}, u32[]{:S(2)}) copy-start(f32[1,512]{1,0:T(1,128)S(1)} %get-tuple-element.143) | copy-start | bytes 6148
  14.4 9.7 %copy-start.15 = (f32[1,512]{1,0:T(1,128)}, f32[1,512]{1,0:T(1,128)S(1)}, u32[]{:S(2)}) copy-start(f32[1,512]{1,0:T(1,128)S(1)} %get-tuple-element.144) | copy-start | bytes 6148
  14.4 9.7 %copy-start.17 = (f32[1,512]{1,0:T(1,128)}, f32[1,512]{1,0:T(1,128)S(1)}, u32[]{:S(2)}) copy-start(f32[1,512]{1,0:T(1,128)S(1)} %get-tuple-element.145) | copy-start | bytes 6148
  14.4 9.7 %copy-start.19 = (f32[1,512]{1,0:T(1,128)}, f32[1,512]{1,0:T(1,128)S(1)}, u32[]{:S(2)}) copy-start(f32[1,512]{1,0:T(1,128)S(1)} %get-tuple-element.146) | copy-start | bytes 6148
  22.5 42.7 %collective-permute-start.3 = (bf16[1024,512]{1,0:T(8,128)(2,1)}, bf16[1024,512]{1,0:T(8,128)(2,1)}, u32[]{:S(2)}, u32[]{:S(2)}) collective-permute-start(bf16[1024,512]{1,0:T(8,128)(2,1)} %pad_maximum_fusion.10), channel_id=1, source_target_pairs={{0,2},{1,3},{2,0},{3,1},{4,6},{5,7},{6,4},{7,5},{8,10},{9,11},{10,... | collective-permute-start | bytes 3145736 | tf_op jit(solution)/shard_map/ppermute | solution.py:31
  28.8 48.8 %copy-start.21 = (f32[256]{0:T(256)}, f32[256]{0:T(256)S(1)}, u32[]{:S(2)}) copy-start(f32[256]{0:T(256)S(1)} %div.15) | copy-start | bytes 3076
  29.1 48.4 %copy-start.22 = (f32[256]{0:T(256)}, f32[256]{0:T(256)S(1)}, u32[]{:S(2)}) copy-start(f32[256]{0:T(256)S(1)} %rsqrt.13) | copy-start | bytes 3076
  29.1 39.1 %copy-start.59 = (f32[512]{0:T(512)S(1)}, f32[512]{0:T(512)}, u32[]{:S(2)}) copy-start(f32[512]{0:T(512)} %param.10) | copy-start | bytes 6148
  68.2 2.6 %copy-start.7 = (bf16[1,32,8,512]{3,2,1,0:T(8,128)(2,1)S(1)}, bf16[1,32,8,512]{3,2,1,0:T(8,128)(2,1)}, u32[]{:S(2)}) copy-start(bf16[1,32,8,512]{3,2,1,0:T(8,128)(2,1)} %param.13) | copy-start | bytes 786436
  68.2 2.6 %copy-start.3 = (bf16[1024,512]{1,0:T(8,128)(2,1)S(1)}, bf16[1024,512]{1,0:T(8,128)(2,1)}, u32[]{:S(2)}) copy-start(bf16[1024,512]{1,0:T(8,128)(2,1)} %get-tuple-element.66) | copy-start | bytes 3145732
  68.2 2.6 %copy-start.5 = (bf16[1024,512]{1,0:T(8,128)(2,1)S(1)}, bf16[1024,512]{1,0:T(8,128)(2,1)}, u32[]{:S(2)}) copy-start(bf16[1024,512]{1,0:T(8,128)(2,1)} %get-tuple-element.67) | copy-start | bytes 3145732
  77.6 2.8 %copy-start.60 = (f32[512]{0:T(512)S(1)}, f32[512]{0:T(512)}, u32[]{:S(2)}) copy-start(f32[512]{0:T(512)} %param.10) | copy-start | bytes 6148
  86.9 2.2 copy-start.8
  89.1 1.1 copy-start.23
  89.1 1.1 copy-start.24
  89.1 1.1 copy-start.25
  89.1 1.1 copy-start.26
  89.1 1.1 copy-start.27
  89.1 1.1 copy-start.28
  89.1 1.1 copy-start.29
  89.1 1.1 copy-start.30
  89.1 1.1 copy-start.31
  89.1 1.1 copy-start.32
  93.0 2.8 %copy-start = (bf16[2,2,1088,512]{3,2,1,0:T(8,128)(2,1)}, bf16[2,2,1088,512]{3,2,1,0:T(8,128)(2,1)S(1)}, u32[]{:S(2)}) copy-start(bf16[2,2,1088,512]{3,2,1,0:T(8,128)(2,1)S(1)} %copy.23) | copy-start | bytes 13369348
  93.0 4.2 %copy-start.12 = (f32[1,512]{1,0:T(1,128)S(1)}, f32[1,512]{1,0:T(1,128)}, u32[]{:S(2)}) copy-start(f32[1,512]{1,0:T(1,128)} %copy-done.11) | copy-start | bytes 6148
  93.0 4.2 %copy-start.14 = (f32[1,512]{1,0:T(1,128)S(1)}, f32[1,512]{1,0:T(1,128)}, u32[]{:S(2)}) copy-start(f32[1,512]{1,0:T(1,128)} %copy-done.13) | copy-start | bytes 6148
  93.0 4.2 %copy-start.16 = (f32[1,512]{1,0:T(1,128)S(1)}, f32[1,512]{1,0:T(1,128)}, u32[]{:S(2)}) copy-start(f32[1,512]{1,0:T(1,128)} %copy-done.15) | copy-start | bytes 6148
  93.0 4.2 %copy-start.18 = (f32[1,512]{1,0:T(1,128)S(1)}, f32[1,512]{1,0:T(1,128)}, u32[]{:S(2)}) copy-start(f32[1,512]{1,0:T(1,128)} %copy-done.17) | copy-start | bytes 6148
  93.0 4.2 %copy-start.20 = (f32[1,512]{1,0:T(1,128)S(1)}, f32[1,512]{1,0:T(1,128)}, u32[]{:S(2)}) copy-start(f32[1,512]{1,0:T(1,128)} %copy-done.19) | copy-start | bytes 6148
  95.8 5.0 %collective-permute-start.6 = (bf16[2176,512]{1,0:T(8,128)(2,1)}, bf16[2176,512]{1,0:T(8,128)(2,1)}, u32[]{:S(2)}, u32[]{:S(2)}) collective-permute-start(bf16[2176,512]{1,0:T(8,128)(2,1)} %constant_dynamic-slice_fusion), channel_id=1, source_target_pairs={{0,1},{1,0},{2,3},{3,2},{4,5},{5,4},{6,7},{7,6},{8,9},{9,8},{10,11... | collective-permute-start | bytes 6684680 | tf_op jit(solution)/shard_map/ppermute | solution.py:31
  98.1 2.7 %slice-start = ((s8[4456448]{0:T(1024)(128)(4,1)}), s8[4194304]{0:T(1024)(128)(4,1)S(1)}, s32[]{:S(2)}) async-start(s8[4456448]{0:T(1024)(128)(4,1)} %bitcast.266), calls=%async_computation.1 | async-start | bytes 8388608
  99.5 1.3 slice-start.1
  103.2 27.0 %collective-permute-start.7 = (bf16[1088,512]{1,0:T(8,128)(2,1)S(1)}, bf16[1088,512]{1,0:T(8,128)(2,1)S(1)}, u32[]{:S(2)}, u32[]{:S(2)}) collective-permute-start(bf16[1088,512]{1,0:T(8,128)(2,1)S(1)} %dynamic-slice_convert_fusion), channel_id=1, source_target_pairs={{0,2},{1,3},{2,0},{3,1},{4,6},{5,7},{6,4},{7,5},{8,10},{9,11},{10,... | collective-permute-start | bytes 3342344 | tf_op jit(solution)/shard_map/ppermute | solution.py:31
  104.9 7.0 %copy-start.9 = (bf16[1,32,8,512]{3,2,1,0:T(8,128)(2,1)S(1)}, bf16[1,32,8,512]{3,2,1,0:T(8,128)(2,1)}, u32[]{:S(2)}) copy-start(bf16[1,32,8,512]{3,2,1,0:T(8,128)(2,1)} %param.13) | copy-start | bytes 786436
  130.2 4.1 %copy-start.6 = (bf16[1024,512]{1,0:T(8,128)(2,1)S(1)}, bf16[1024,512]{1,0:T(8,128)(2,1)}, u32[]{:S(2)}) copy-start(bf16[1024,512]{1,0:T(8,128)(2,1)} %get-tuple-element.67) | copy-start | bytes 3145732
  130.5 3.7 %copy-start.2 = (bf16[1,32,8,512]{3,2,1,0:T(8,128)(2,1)S(1)}, bf16[1,32,8,512]{3,2,1,0:T(8,128)(2,1)}, u32[]{:S(2)}) copy-start(bf16[1,32,8,512]{3,2,1,0:T(8,128)(2,1)} %param.7) | copy-start | bytes 786436
  130.6 3.7 %copy-start.4 = (bf16[1024,512]{1,0:T(8,128)(2,1)S(1)}, bf16[1024,512]{1,0:T(8,128)(2,1)}, u32[]{:S(2)}) copy-start(bf16[1024,512]{1,0:T(8,128)(2,1)} %get-tuple-element.66) | copy-start | bytes 3145732
  130.7 11.2 %collective-permute-start.8 = (bf16[272,512]{1,0:T(8,128)(2,1)S(1)}, bf16[272,512]{1,0:T(8,128)(2,1)S(1)}, u32[]{:S(2)}, u32[]{:S(2)}) collective-permute-start(bf16[272,512]{1,0:T(8,128)(2,1)S(1)} %get-tuple-element.63), channel_id=1, source_target_pairs={{0,8},{4,12},{8,0},{12,4},{16,24},{20,28},{24,16},{28,20},{32,40},... | collective-permute-start | bytes 835592 | tf_op jit(solution)/shard_map/ppermute | solution.py:78
  131.7 14.7 %collective-permute-start.10 = (bf16[272,512]{1,0:T(8,128)(2,1)S(1)}, bf16[272,512]{1,0:T(8,128)(2,1)S(1)}, u32[]{:S(2)}, u32[]{:S(2)}) collective-permute-start(bf16[272,512]{1,0:T(8,128)(2,1)S(1)} %get-tuple-element.64), channel_id=1, source_target_pairs={{0,12},{4,8},{8,4},{12,0},{16,28},{20,24},{24,20},{28,16},{32,44},... | collective-permute-start | bytes 835592 | tf_op jit(solution)/shard_map/ppermute | solution.py:78
  132.8 13.6 %collective-permute-start.9 = (bf16[272,512]{1,0:T(8,128)(2,1)S(1)}, bf16[272,512]{1,0:T(8,128)(2,1)S(1)}, u32[]{:S(2)}, u32[]{:S(2)}) collective-permute-start(bf16[272,512]{1,0:T(8,128)(2,1)S(1)} %get-tuple-element.65), channel_id=1, source_target_pairs={{0,4},{4,0},{8,12},{12,8},{16,20},{20,16},{24,28},{28,24},{32,36},... | collective-permute-start | bytes 835592 | tf_op jit(solution)/shard_map/ppermute | solution.py:78
  146.6 8.0 %collective-permute-start.11 = (bf16[68,512]{1,0:T(8,128)(2,1)S(1)}, bf16[68,512]{1,0:T(8,128)(2,1)S(1)}, u32[]{:S(2)}, u32[]{:S(2)}) collective-permute-start(bf16[68,512]{1,0:T(8,128)(2,1)S(1)} %get-tuple-element.76), channel_id=1, source_target_pairs={{0,32},{4,36},{8,40},{12,44},{16,48},{20,52},{24,56},{28,60},{32,0... | collective-permute-start | bytes 208904 | tf_op jit(solution)/shard_map/ppermute | solution.py:78
  150.0 6.7 %collective-permute-start.13 = (bf16[68,512]{1,0:T(8,128)(2,1)S(1)}, bf16[68,512]{1,0:T(8,128)(2,1)S(1)}, u32[]{:S(2)}, u32[]{:S(2)}) collective-permute-start(bf16[68,512]{1,0:T(8,128)(2,1)S(1)} %get-tuple-element.77), channel_id=1, source_target_pairs={{0,48},{4,52},{8,56},{12,60},{16,32},{20,36},{24,40},{28,44},{32,1... | collective-permute-start | bytes 208904 | tf_op jit(solution)/shard_map/ppermute | solution.py:78
  150.0 6.7 %collective-permute-start.12 = (bf16[68,512]{1,0:T(8,128)(2,1)S(1)}, bf16[68,512]{1,0:T(8,128)(2,1)S(1)}, u32[]{:S(2)}, u32[]{:S(2)}) collective-permute-start(bf16[68,512]{1,0:T(8,128)(2,1)S(1)} %get-tuple-element.78), channel_id=1, source_target_pairs={{0,16},{4,20},{8,24},{12,28},{16,0},{20,4},{24,8},{28,12},{32,48},... | collective-permute-start | bytes 208904 | tf_op jit(solution)/shard_map/ppermute | solution.py:78
  156.8 9.5 %collective-permute-start.14 = (bf16[17,512]{1,0:T(8,128)(2,1)S(1)}, bf16[17,512]{1,0:T(8,128)(2,1)S(1)}, u32[]{:S(2)}, u32[]{:S(2)}) collective-permute-start(bf16[17,512]{1,0:T(8,128)(2,1)S(1)} %get-tuple-element.130), channel_id=1, source_target_pairs={{0,128},{4,132},{8,136},{12,140},{16,144},{20,148},{24,152},{28,15... | collective-permute-start | bytes 52232 | tf_op jit(solution)/shard_map/ppermute | solution.py:78
  159.8 10.1 %collective-permute-start.16 = (bf16[17,512]{1,0:T(8,128)(2,1)S(1)}, bf16[17,512]{1,0:T(8,128)(2,1)S(1)}, u32[]{:S(2)}, u32[]{:S(2)}) collective-permute-start(bf16[17,512]{1,0:T(8,128)(2,1)S(1)} %get-tuple-element.131), channel_id=1, source_target_pairs={{0,192},{4,196},{8,200},{12,204},{16,208},{20,212},{24,216},{28,22... | collective-permute-start | bytes 52232 | tf_op jit(solution)/shard_map/ppermute | solution.py:78
  165.9 8.0 %collective-permute-start.15 = (bf16[17,512]{1,0:T(8,128)(2,1)S(1)}, bf16[17,512]{1,0:T(8,128)(2,1)S(1)}, u32[]{:S(2)}, u32[]{:S(2)}) collective-permute-start(bf16[17,512]{1,0:T(8,128)(2,1)S(1)} %get-tuple-element.132), channel_id=1, source_target_pairs={{0,64},{4,68},{8,72},{12,76},{16,80},{20,84},{24,88},{28,92},{32,9... | collective-permute-start | bytes 52232 | tf_op jit(solution)/shard_map/ppermute | solution.py:78
  173.9 14.4 %collective-permute-start.19 = (bf16[17,512]{1,0:T(8,128)(2,1)S(1)}, bf16[17,512]{1,0:T(8,128)(2,1)S(1)}, u32[]{:S(2)}, u32[]{:S(2)}) collective-permute-start(bf16[17,512]{1,0:T(8,128)(2,1)S(1)} %add_convert_fusion), channel_id=1, source_target_pairs={{0,192},{4,196},{8,200},{12,204},{16,208},{20,212},{24,216},{28,22... | collective-permute-start | bytes 52232 | tf_op jit(solution)/shard_map/ppermute | solution.py:78
  176.9 11.1 %collective-permute-start.18 = (bf16[17,512]{1,0:T(8,128)(2,1)S(1)}, bf16[17,512]{1,0:T(8,128)(2,1)S(1)}, u32[]{:S(2)}, u32[]{:S(2)}) collective-permute-start(bf16[17,512]{1,0:T(8,128)(2,1)S(1)} %add_convert_fusion), channel_id=1, source_target_pairs={{0,64},{4,68},{8,72},{12,76},{16,80},{20,84},{24,88},{28,92},{32,9... | collective-permute-start | bytes 52232 | tf_op jit(solution)/shard_map/ppermute | solution.py:78
  182.3 5.3 %collective-permute-start.17 = (bf16[17,512]{1,0:T(8,128)(2,1)S(1)}, bf16[17,512]{1,0:T(8,128)(2,1)S(1)}, u32[]{:S(2)}, u32[]{:S(2)}) collective-permute-start(bf16[17,512]{1,0:T(8,128)(2,1)S(1)} %add_convert_fusion), channel_id=1, source_target_pairs={{0,128},{4,132},{8,136},{12,140},{16,144},{20,148},{24,152},{28,15... | collective-permute-start | bytes 52232 | tf_op jit(solution)/shard_map/ppermute | solution.py:78
  183.1 16.6 %collective-permute-start.5 = (bf16[1,32,3,512]{3,2,1,0:T(4,128)(2,1)S(1)}, bf16[1,32,3,512]{3,2,1,0:T(4,128)(2,1)S(1)}, u32[]{:S(2)}, u32[]{:S(2)}) collective-permute-start(bf16[1,32,3,512]{3,2,1,0:T(4,128)(2,1)S(1)} %fusion.101), channel_id=1, source_target_pairs={{4,0},{8,4},{12,8},{16,12},{20,16},{24,20},{28,24},{32,28},{36,32}... | collective-permute-start | bytes 294920 | tf_op jit(solution)/shard_map/ppermute | solution.py:22
  184.1 15.5 %collective-permute-start.4 = (bf16[1,32,3,512]{3,2,1,0:T(4,128)(2,1)S(1)}, bf16[1,32,3,512]{3,2,1,0:T(4,128)(2,1)S(1)}, u32[]{:S(2)}, u32[]{:S(2)}) collective-permute-start(bf16[1,32,3,512]{3,2,1,0:T(4,128)(2,1)S(1)} %fusion.100), channel_id=1, source_target_pairs={{0,4},{4,8},{8,12},{12,16},{16,20},{20,24},{24,28},{28,32},{32,36}... | collective-permute-start | bytes 294920 | tf_op jit(solution)/shard_map/ppermute | solution.py:20
  188.6 8.7 %collective-permute-start.22 = (bf16[68,512]{1,0:T(8,128)(2,1)S(1)}, bf16[68,512]{1,0:T(8,128)(2,1)S(1)}, u32[]{:S(2)}, u32[]{:S(2)}) collective-permute-start(bf16[68,512]{1,0:T(8,128)(2,1)S(1)} %dynamic_update_slice.39), channel_id=1, source_target_pairs={{0,48},{4,52},{8,56},{12,60},{16,32},{20,36},{24,40},{28,44},{32,1... | collective-permute-start | bytes 208904 | tf_op jit(solution)/shard_map/ppermute | solution.py:78
  188.9 7.8 %collective-permute-start.21 = (bf16[68,512]{1,0:T(8,128)(2,1)S(1)}, bf16[68,512]{1,0:T(8,128)(2,1)S(1)}, u32[]{:S(2)}, u32[]{:S(2)}) collective-permute-start(bf16[68,512]{1,0:T(8,128)(2,1)S(1)} %dynamic_update_slice.39), channel_id=1, source_target_pairs={{0,16},{4,20},{8,24},{12,28},{16,0},{20,4},{24,8},{28,12},{32,48},... | collective-permute-start | bytes 208904 | tf_op jit(solution)/shard_map/ppermute | solution.py:78
  191.0 5.3 %collective-permute-start.20 = (bf16[68,512]{1,0:T(8,128)(2,1)S(1)}, bf16[68,512]{1,0:T(8,128)(2,1)S(1)}, u32[]{:S(2)}, u32[]{:S(2)}) collective-permute-start(bf16[68,512]{1,0:T(8,128)(2,1)S(1)} %dynamic_update_slice.39), channel_id=1, source_target_pairs={{0,32},{4,36},{8,40},{12,44},{16,48},{20,52},{24,56},{28,60},{32,0... | collective-permute-start | bytes 208904 | tf_op jit(solution)/shard_map/ppermute | solution.py:78
  198.1 8.9 %collective-permute-start.23 = (bf16[272,512]{1,0:T(8,128)(2,1)S(1)}, bf16[272,512]{1,0:T(8,128)(2,1)S(1)}, u32[]{:S(2)}, u32[]{:S(2)}) collective-permute-start(bf16[272,512]{1,0:T(8,128)(2,1)S(1)} %dynamic_update_slice.43), channel_id=1, source_target_pairs={{0,8},{4,12},{8,0},{12,4},{16,24},{20,28},{24,16},{28,20},{32,40},... | collective-permute-start | bytes 835592 | tf_op jit(solution)/shard_map/ppermute | solution.py:78
  200.0 9.6 %collective-permute-start.24 = (bf16[272,512]{1,0:T(8,128)(2,1)S(1)}, bf16[272,512]{1,0:T(8,128)(2,1)S(1)}, u32[]{:S(2)}, u32[]{:S(2)}) collective-permute-start(bf16[272,512]{1,0:T(8,128)(2,1)S(1)} %dynamic_update_slice.43), channel_id=1, source_target_pairs={{0,4},{4,0},{8,12},{12,8},{16,20},{20,16},{24,28},{28,24},{32,36},... | collective-permute-start | bytes 835592 | tf_op jit(solution)/shard_map/ppermute | solution.py:78
  203.4 7.8 %collective-permute-start.25 = (bf16[272,512]{1,0:T(8,128)(2,1)S(1)}, bf16[272,512]{1,0:T(8,128)(2,1)S(1)}, u32[]{:S(2)}, u32[]{:S(2)}) collective-permute-start(bf16[272,512]{1,0:T(8,128)(2,1)S(1)} %dynamic_update_slice.43), channel_id=1, source_target_pairs={{0,12},{4,8},{8,4},{12,0},{16,28},{20,24},{24,20},{28,16},{32,44},... | collective-permute-start | bytes 835592 | tf_op jit(solution)/shard_map/ppermute | solution.py:78
  (31 other events, 33.7 us)
Sparse Core Ops, SparseCore 0:
  9.8 51.2 all-gather.1
where the time goes:
time: 225 us; the launch traced here: 221 us
  waiting for transfers between devices  90.9 us (40%)
  starting transfers between devices  44.4 us (20%)
  other arithmetic  31.6 us (14%)
  local copies, waits for them, and re-layouts  21.2 us (9%)
  between operations  19.3 us (9%)
  matrix products  13.8 us (6%)
    ppermute x4, waiting for transfers between devices, exchange(): return lax.ppermute(value, axis, [(i, i ^ 1 << bit) for i in range(count)])  54.3 us
    ppermute x18, waiting for transfers between devices, swapped(): return lax.ppermute(value, axis, [(i, i ^ mask) for i in range(count)])  35.9 us
    ppermute x18, starting transfers between devices, swapped(): return lax.ppermute(value, axis, [(i, i ^ mask) for i in range(count)])  34.6 us
    add_any x1, other arithmetic, depthwise(): padded[:, row:row + height, col:col + width, :] * kernel[7 * row + col]  6.72 us
    reduce_sum x3, other arithmetic, depthwise(): padded[:, row:row + height, col:col + width, :] * kernel[7 * row + col]  5.77 us
    reduce_sum x1, other arithmetic, body(): mean = jnp.mean(rows, axis=-1, keepdims=True)  4.6 us
  transfers between devices with their start and end apart: 27, of which 13 were waited for; matrix products, arithmetic and copies ran while one was open for 15% of the time, Pallas kernels for 0%

commit v1 on v0

--- a/solution.py
+++ b/solution.py
@@ -78,15 +78,14 @@
     return lax.ppermute(value, axis, [(i, i ^ mask) for i in range(count)])
 
 
-def gathered_rows(shard):
+def gathered(shard):
     me = lax.axis_index("fsdp")
-    for bit in (0, 1):
-        side = (me >> bit) & 1
-        got = exchange(shard, "fsdp", bit)
-        shard = jnp.concatenate(
-            [jnp.where(side == 0, shard, got), jnp.where(side == 0, got, shard)], axis=0
-        )
-    return shard
+    high, low = (me >> 1) & 1, me & 1
+    got = exchange(shard, "fsdp", 1)
+    pair = jnp.stack([jnp.where(high == 0, shard, got), jnp.where(high == 0, got, shard)])
+    other = exchange(pair, "fsdp", 0)
+    first, second = jnp.where(low == 0, pair, other), jnp.where(low == 0, other, pair)
+    return jnp.stack([first, second], axis=1).reshape((4,) + shard.shape)
 
 
 def gelu(value):
@@ -140,10 +139,9 @@
     scaled = (normed * gain).astype(jnp.bfloat16)
     back = cotangent.reshape(count, channels)
     contract_last = (((1,), (1,)), ((), ()))
-    full_in, full_out = (
-        lax.all_gather(w_in, "fsdp", axis=1, tiled=True),
-        gathered_rows(w_out),
-    )
+    both = gathered(jnp.stack([w_in, w_out]))
+    full_in = jnp.moveaxis(both[:, 0], 0, 1).reshape(w_in.shape[0], -1)
+    full_out = both[:, 1].reshape(-1, w_out.shape[1])
     pre = jnp.dot(scaled, full_in, preferred_element_type=jnp.float32)
     hidden = gelu(pre).astype(jnp.bfloat16)
     branch = jnp.dot(hidden, full_out, preferred_element_type=jnp.float32)

time: 225 us -> 202 us (0.90)
  the two profiles are of different devices: /device:TPU:32 before, /device:TPU:8 now
where the time goes in v1:
time: 202 us; the launch traced here: 199 us
  waiting for transfers between devices  66.3 us (33%)
  starting transfers between devices  51.9 us (26%)
  other arithmetic  37.3 us (18%)
  local copies, waits for them, and re-layouts  25.5 us (13%)
  matrix products  11.1 us (5%)
  between operations  6.88 us (3%)
    ppermute x18, starting transfers between devices, swapped(): return lax.ppermute(value, axis, [(i, i ^ mask) for i in range(count)])  35.8 us
    ppermute x4, waiting for transfers between devices, exchange(): return lax.ppermute(value, axis, [(i, i ^ 1 << bit) for i in range(count)])  33.6 us
    ppermute x18, waiting for transfers between devices, swapped(): return lax.ppermute(value, axis, [(i, i ^ mask) for i in range(count)])  32.6 us
    ppermute x2, starting transfers between devices, extended(): lax.ppermute(head, axis, [((i + 1) % count, i) for i in range(count)])  12.8 us
    add_any x1, other arithmetic, depthwise(): padded[:, row:row + height, col:col + width, :] * kernel[7 * row + col]  6.73 us
    reduce_sum x1, other arithmetic, body(): mean = jnp.mean(rows, axis=-1, keepdims=True)  6.26 us
    reduce_sum x3, other arithmetic, depthwise(): padded[:, row:row + height, col:col + width, :] * kernel[7 * row + col]  5.39 us
  transfers between devices with their start and end apart: 26, of which 11 were waited for; matrix products, arithmetic and copies ran while one was open for 17% of the time, Pallas kernels for 0%

profile of v1, /device:TPU:8, one launch (start us, length us, event | category | flops | bytes accessed | tf_op | source)
XLA Modules:
  0.0 198.9 jit_solution(10487106111413623576)
XLA Ops:
  0.7 1.4 pad_maximum_fusion.3
  2.1 2.2 %collective-permute-start.2 = (bf16[2,512,512]{2,1,0:T(8,128)(2,1)S(1)}, bf16[2,512,512]{2,1,0:T(8,128)(2,1)}, u32[]{:S(2)}, u32[]{:S(2)}) collective-permute-start(bf16[2,512,512]{2,1,0:T(8,128)(2,1)S(1)} %pad_maximum_fusion.3), channel_id=1, source_target_pairs={{0,2},{1,3},{2,0},{3,1},{4,6},{5,7},{6,4},{7,5},{8,10},{9,11},{10,... | collective-permute-start | bytes 3145736 | tf_op jit(solution)/shard_map/ppermute | solution.py:31
  4.3 0.7 fusion.111
  5.1 8.4 %collective-permute-start.1 = (bf16[1,32,3,512]{3,2,1,0:T(4,128)(2,1)S(1)}, bf16[1,32,3,512]{3,2,1,0:T(4,128)(2,1)S(1)}, u32[]{:S(2)}, u32[]{:S(2)}) collective-permute-start(bf16[1,32,3,512]{3,2,1,0:T(4,128)(2,1)S(1)} %get-tuple-element.131), channel_id=1, source_target_pairs={{4,0},{8,4},{12,8},{16,12},{20,16},{24,20},{28,24},{32,28},{36,32}... | collective-permute-start | bytes 294920 | tf_op jit(solution)/shard_map/ppermute | solution.py:22
  14.1 0.7 fusion.112
  14.7 0.7 fusion.113
  15.4 14.6 %collective-permute-done.2 = bf16[2,512,512]{2,1,0:T(8,128)(2,1)} collective-permute-done((bf16[2,512,512]{2,1,0:T(8,128)(2,1)S(1)}, bf16[2,512,512]{2,1,0:T(8,128)(2,1)}, u32[]{:S(2)}, u32[]{:S(2)}) %collective-permute-start.2) | collective-permute-done | bytes 1048608 | tf_op jit(solution)/shard_map/ppermute | solution.py:31
  30.0 1.4 select_bitcast_fusion.3
  31.4 1.5 pad_maximum_fusion.2
  37.3 1.2 fusion.104
  38.9 6.3 %fusion.106 = (f32[32,8]{1,0:T(8,128)S(1)}, f32[1,32,8,512]{3,2,1,0:T(8,128)}) fusion(f32[512]{0:T(512)S(1)} %bitcast.317, bf16[1,38,14,512]{3,2,1,0:T(8,128)(2,1)S(1)} %get-tuple-element.60, f32[512]{0:T(512)S(1)} %bitcast.335, f32[512]{0:T(512)S(1)} %bitcast.371, f32[512]{0:T(512)S(1)} %bitcast.373, f32[512]{0:T(512)S(1)} %bitcast.375, ...), kind=kLoop, calls=%fused_computation.281 | loop fusion | flops 21626624 | bytes 12094464 | tf_op jit(solution)/shard_map/reduce_sum | solution.py:135
  45.3 1.2 multiply_reduce_fusion.2
  46.6 1.9 select_bitcast_fusion.1
  48.9 2.4 %fusion.108 = (bf16[4,1,512,512]{3,2,1,0:T(8,128)(2,1)}, bf16[512,4,512]{2,0,1:T(8,128)(2,1)}) fusion(bf16[4,2,512,512]{3,2,1,0:T(8,128)(2,1)S(1)} %bitcast.289), kind=kLoop, calls=%fused_computation.282 | loop fusion | bytes 8388608 | tf_op jit(solution)/shard_map/slice | solution.py:144
  51.4 2.8 %copy.19 = bf16[512,4,512]{0,2,1:T(8,128)(2,1)S(1)} copy(bf16[512,4,512]{2,0,1:T(8,128)(2,1)} %get-tuple-element.64) | data formatting | bytes 4194304 | tf_op jit(solution)/shard_map/transpose | solution.py:143
  54.2 3.0 %multiply_convert_fusion.2 = (bf16[256,2048]{1,0:T(8,128)(2,1)}, f32[256,2048]{1,0:T(8,128)S(1)}) fusion(bf16[512,2048]{0,1:T(8,128)(2,1)S(1)} %bitcast.290, f32[512]{0:T(512)S(1)} %copy-done.111, f32[32,8]{1,0:T(8,128)S(1)} %add_rsqrt_fusion, f32[1,32,8,512]{3,2,1,0:T(8,128)} %get-tuple-element.62, f32[32,8]{1,0:T(8,128)S(1)} %broadcast_multiply_fusion), kind=kOutput, calls=%fused_computation.17 | convolution fusion | flops 540016640 | bytes 5771264 | tf_op jit(solution)/shard_map/dot_general | solution.py:145
  57.2 2.1 %fusion.1 = bf16[256,2048]{1,0:T(8,128)(2,1)} fusion(bf16[2048,512]{1,0:T(8,128)(2,1)S(1)} %bitcast.297, f32[256,2048]{1,0:T(8,128)S(1)} %get-tuple-element.187, bf16[1,32,8,512]{3,2,1,0:T(8,128)(2,1)S(1)} %copy-done.12), kind=kOutput, calls=%fused_computation.8 | convolution fusion | flops 542113792 | bytes 5505024 | tf_op jit(solution)/shard_map/dot_general | solution.py:148
  59.2 2.6 %reshape.1319 = bf16[256,2,2,512]{3,2,1,0:T(2,128)(2,1)} reshape(bf16[256,2048]{1,0:T(8,128)(2,1)} %fusion.1) | data formatting | bytes 2097152 | tf_op jit(solution)/shard_map/reshape | solution.py:182
  61.8 2.3 %multiply_reduce_fusion = (f32[512]{0:T(512)S(1)}, f32[256]{0:T(256)S(1)}, f32[256]{0:T(256)S(1)}, f32[256,512]{1,0:T(8,128)S(1)}) fusion(f32[1,32,8,512]{3,2,1,0:T(8,128)} %get-tuple-element.62, f32[256]{0:T(256)S(1)} %rsqrt.13, f32[256]{0:T(256)S(1)} %div.17, f32[512]{0:T(512)S(1)} %copy-done.111, bf16[256,2048]{1,0:T(8,128)(2,1)} %fusion.1, ...), kind=kOutput, calls=%fused_computation.230 | convolution fusion | flops 537918464 | bytes 4202496 | tf_op jit(solution)/shard_map/dot_general | solution.py:152
  64.1 2.3 %fusion.87 = (f32[512]{0:T(512)}, f32[512]{0:T(512)}, f32[512]{0:T(512)}, f32[512]{0:T(512)}, f32[512]{0:T(512)}, /*index=5*/f32[512]{0:T(512)}, f32[512]{0:T(51...) fusion(f32[1,38,14,512]{3,2,1,0:T(8,128)S(1)} %get-tuple-elemen, ...), kind=kLoop, calls=%fused_computation.173 | loop fusion | flops 4318720 | bytes 8421376 | tf_op jit(solution)/shard_map/transpose(jvp())/reduce_sum | solution.py:114
  66.4 1.5 fusion.88
  67.9 1.6 fusion.89
  69.5 1.8 copy.30
  71.4 1.6 fusion.5
  73.4 0.7 fusion.6
  74.5 1.0 multiply_convert_fusion.4
  77.0 1.8 constant_dynamic-slice_fusion
  78.8 0.9 copy-done
  81.6 0.9 bitcast_multiply_fusion.46
  82.6 1.3 bitcast_multiply_fusion.47
  83.9 1.3 bitcast_multiply_fusion.48
  85.3 2.3 %convert_add_fusion = bf16[2176,512]{1,0:T(8,128)(2,1)S(1)} fusion(bf16[2176,512]{1,0:T(8,128)(2,1)} %collective-permute-done.6, bf16[4352,512]{1,0:T(8,128)(2,1)S(1)} %bitcast.288, s32[]{:T(128)S(6)} %select_n.106), kind=kLoop, calls=%fused_computation.1 | loop fusion | flops 4456448 | bytes 6684676 | tf_op jit(solution)/shard_map/add | solution.py:42
  88.0 6.7 %pad_add_fusion = f32[1,38,14,512]{3,2,1,0:T(8,128)S(1)} fusion(f32[1,32,8,512]{3,2,1,0:T(8,128)S(1)} %get-tuple-element.82, f32[1,32,8,512]{3,2,1,0:T(8,128)S(1)} %get-tuple-element.83, f32[1,32,8,512]{3,2,1,0:T(8,128)S(1)} %get-tuple-element.84, f32[1,32,8,512]{3,2,1,0:T(8,128)S(1)} %get-tuple-element.85, f32[1,32,8,512]{3,2,1,0:T(8,128)S(1)} %get-tuple-element.86, ...), kind=kLoop, calls=%fused_computation.25 | loop fusion | flops 13074432 | bytes 26779648 | tf_op jit(solution)/shard_map/transpose(jvp())/add_any | solution.py:114
  95.1 19.1 %collective-permute-done.7 = bf16[1088,512]{1,0:T(8,128)(2,1)S(1)} collective-permute-done((bf16[1088,512]{1,0:T(8,128)(2,1)S(1)}, bf16[1088,512]{1,0:T(8,128)(2,1)S(1)}, u32[]{:S(2)}, u32[]{:S(2)}) %collective-permute-start.7) | collective-permute-done | bytes 1114144 | tf_op jit(solution)/shard_map/ppermute | solution.py:31
  115.0 1.1 collective-permute-start.10
  116.1 2.1 %collective-permute-start.9 = (bf16[272,512]{1,0:T(8,128)(2,1)S(1)}, bf16[272,512]{1,0:T(8,128)(2,1)S(1)}, u32[]{:S(2)}, u32[]{:S(2)}) collective-permute-start(bf16[272,512]{1,0:T(8,128)(2,1)S(1)} %get-tuple-element.69), channel_id=1, source_target_pairs={{0,4},{4,0},{8,12},{12,8},{16,20},{20,16},{24,28},{28,24},{32,36},... | collective-permute-start | bytes 835592 | tf_op jit(solution)/shard_map/ppermute | solution.py:78
  118.3 1.4 fusion.9
  119.7 6.1 %collective-permute-done.8 = bf16[272,512]{1,0:T(8,128)(2,1)S(1)} collective-permute-done((bf16[272,512]{1,0:T(8,128)(2,1)S(1)}, bf16[272,512]{1,0:T(8,128)(2,1)S(1)}, u32[]{:S(2)}, u32[]{:S(2)}) %collective-permute-start.8) | collective-permute-done | bytes 278560 | tf_op jit(solution)/shard_map/ppermute | solution.py:78
  125.8 4.0 %collective-permute-done.10 = bf16[272,512]{1,0:T(8,128)(2,1)S(1)} collective-permute-done((bf16[272,512]{1,0:T(8,128)(2,1)S(1)}, bf16[272,512]{1,0:T(8,128)(2,1)S(1)}, u32[]{:S(2)}, u32[]{:S(2)}) %collective-permute-start.10) | collective-permute-done | bytes 278560 | tf_op jit(solution)/shard_map/ppermute | solution.py:78
  130.0 1.1 collective-permute-start.11
  131.2 1.4 collective-permute-start.13
  132.6 1.3 collective-permute-start.12
  134.0 4.1 %collective-permute-done.11 = bf16[68,512]{1,0:T(8,128)(2,1)S(1)} collective-permute-done((bf16[68,512]{1,0:T(8,128)(2,1)S(1)}, bf16[68,512]{1,0:T(8,128)(2,1)S(1)}, u32[]{:S(2)}, u32[]{:S(2)}) %collective-permute-start.11) | collective-permute-done | bytes 69664 | tf_op jit(solution)/shard_map/ppermute | solution.py:78
  138.1 1.3 collective-permute-done.12
  139.4 2.4 %collective-permute-start.14 = (bf16[17,512]{1,0:T(8,128)(2,1)S(1)}, bf16[17,512]{1,0:T(8,128)(2,1)S(1)}, u32[]{:S(2)}, u32[]{:S(2)}) collective-permute-start(bf16[17,512]{1,0:T(8,128)(2,1)S(1)} %get-tuple-element.132), channel_id=1, source_target_pairs={{0,128},{4,132},{8,136},{12,140},{16,144},{20,148},{24,152},{28,15... | collective-permute-start | bytes 52232 | tf_op jit(solution)/shard_map/ppermute | solution.py:78
  141.8 5.9 %collective-permute-start.16 = (bf16[17,512]{1,0:T(8,128)(2,1)S(1)}, bf16[17,512]{1,0:T(8,128)(2,1)S(1)}, u32[]{:S(2)}, u32[]{:S(2)}) collective-permute-start(bf16[17,512]{1,0:T(8,128)(2,1)S(1)} %get-tuple-element.133), channel_id=1, source_target_pairs={{0,192},{4,196},{8,200},{12,204},{16,208},{20,212},{24,216},{28,22... | collective-permute-start | bytes 52232 | tf_op jit(solution)/shard_map/ppermute | solution.py:78
  147.7 0.8 collective-permute-start.15
  148.6 3.4 %collective-permute-done.16 = bf16[17,512]{1,0:T(8,128)(2,1)S(1)} collective-permute-done((bf16[17,512]{1,0:T(8,128)(2,1)S(1)}, bf16[17,512]{1,0:T(8,128)(2,1)S(1)}, u32[]{:S(2)}, u32[]{:S(2)}) %collective-permute-start.16) | collective-permute-done | bytes 17440 | tf_op jit(solution)/shard_map/ppermute | solution.py:78
  151.9 3.5 %collective-permute-done.15 = bf16[17,512]{1,0:T(8,128)(2,1)S(1)} collective-permute-done((bf16[17,512]{1,0:T(8,128)(2,1)S(1)}, bf16[17,512]{1,0:T(8,128)(2,1)S(1)}, u32[]{:S(2)}, u32[]{:S(2)}) %collective-permute-start.15) | collective-permute-done | bytes 17440 | tf_op jit(solution)/shard_map/ppermute | solution.py:78
  155.4 2.6 %collective-permute-start.19 = (bf16[17,512]{1,0:T(8,128)(2,1)S(1)}, bf16[17,512]{1,0:T(8,128)(2,1)S(1)}, u32[]{:S(2)}, u32[]{:S(2)}) collective-permute-start(bf16[17,512]{1,0:T(8,128)(2,1)S(1)} %add_convert_fusion), channel_id=1, source_target_pairs={{0,192},{4,196},{8,200},{12,204},{16,208},{20,212},{24,216},{28,22... | collective-permute-start | bytes 52232 | tf_op jit(solution)/shard_map/ppermute | solution.py:78
  158.0 5.2 %collective-permute-start.18 = (bf16[17,512]{1,0:T(8,128)(2,1)S(1)}, bf16[17,512]{1,0:T(8,128)(2,1)S(1)}, u32[]{:S(2)}, u32[]{:S(2)}) collective-permute-start(bf16[17,512]{1,0:T(8,128)(2,1)S(1)} %add_convert_fusion), channel_id=1, source_target_pairs={{0,64},{4,68},{8,72},{12,76},{16,80},{20,84},{24,88},{28,92},{32,9... | collective-permute-start | bytes 52232 | tf_op jit(solution)/shard_map/ppermute | solution.py:78
  163.2 1.2 collective-permute-start.17
  164.6 4.4 %collective-permute-start.5 = (bf16[1,32,3,512]{3,2,1,0:T(4,128)(2,1)S(1)}, bf16[1,32,3,512]{3,2,1,0:T(4,128)(2,1)S(1)}, u32[]{:S(2)}, u32[]{:S(2)}) collective-permute-start(bf16[1,32,3,512]{3,2,1,0:T(4,128)(2,1)S(1)} %fusion.96), channel_id=1, source_target_pairs={{4,0},{8,4},{12,8},{16,12},{20,16},{24,20},{28,24},{32,28},{36,32}... | collective-permute-start | bytes 294920 | tf_op jit(solution)/shard_map/ppermute | solution.py:22
  170.6 1.5 collective-permute-start.22
  172.2 2.9 %collective-permute-start.20 = (bf16[68,512]{1,0:T(8,128)(2,1)S(1)}, bf16[68,512]{1,0:T(8,128)(2,1)S(1)}, u32[]{:S(2)}, u32[]{:S(2)}) collective-permute-start(bf16[68,512]{1,0:T(8,128)(2,1)S(1)} %dynamic_update_slice.39), channel_id=1, source_target_pairs={{0,32},{4,36},{8,40},{12,44},{16,48},{20,52},{24,56},{28,60},{32,0... | collective-permute-start | bytes 208904 | tf_op jit(solution)/shard_map/ppermute | solution.py:78
  175.2 0.7 dynamic_update_slice.40
  175.9 1.8 collective-permute-done.20
  178.4 0.7 dynamic_update_slice.42
  179.6 1.3 collective-permute-start.23
  181.2 4.6 %collective-permute-start.24 = (bf16[272,512]{1,0:T(8,128)(2,1)S(1)}, bf16[272,512]{1,0:T(8,128)(2,1)S(1)}, u32[]{:S(2)}, u32[]{:S(2)}) collective-permute-start(bf16[272,512]{1,0:T(8,128)(2,1)S(1)} %dynamic_update_slice.43), channel_id=1, source_target_pairs={{0,4},{4,0},{8,12},{12,8},{16,20},{20,16},{24,28},{28,24},{32,36},... | collective-permute-start | bytes 835592 | tf_op jit(solution)/shard_map/ppermute | solution.py:78
  185.9 0.9 pad_maximum_fusion.6
  186.9 3.8 %collective-permute-done.23 = bf16[272,512]{1,0:T(8,128)(2,1)S(1)} collective-permute-done((bf16[272,512]{1,0:T(8,128)(2,1)S(1)}, bf16[272,512]{1,0:T(8,128)(2,1)S(1)}, u32[]{:S(2)}, u32[]{:S(2)}) %collective-permute-start.23) | collective-permute-done | bytes 278560 | tf_op jit(solution)/shard_map/ppermute | solution.py:78
  190.7 4.8 %collective-permute-done.24 = bf16[272,512]{1,0:T(8,128)(2,1)S(1)} collective-permute-done((bf16[272,512]{1,0:T(8,128)(2,1)S(1)}, bf16[272,512]{1,0:T(8,128)(2,1)S(1)}, u32[]{:S(2)}, u32[]{:S(2)}) %collective-permute-start.24) | collective-permute-done | bytes 278560 | tf_op jit(solution)/shard_map/ppermute | solution.py:78
  196.8 1.6 fusion.110
  (309 shorter events, 12.1 us)
Async XLA Ops:
  0.6 3.7 %copy-start.4 = (bf16[1,32,8,512]{3,2,1,0:T(8,128)(2,1)S(1)}, bf16[1,32,8,512]{3,2,1,0:T(8,128)(2,1)}, u32[]{:S(2)}) copy-start(bf16[1,32,8,512]{3,2,1,0:T(8,128)(2,1)} %param.7) | copy-start | bytes 786436
  0.6 12.8 %copy-start.14 = (f32[49,512]{1,0:T(8,128)S(1)}, f32[49,512]{1,0:T(8,128)}, u32[]{:S(2)}) copy-start(f32[49,512]{1,0:T(8,128)} %param.9) | copy-start | bytes 301060
  0.7 29.3 %copy-start.7 = (bf16[512,512]{1,0:T(8,128)(2,1)S(1)}, bf16[512,512]{1,0:T(8,128)(2,1)}, u32[]{:S(2)}) copy-start(bf16[512,512]{1,0:T(8,128)(2,1)} %param.12) | copy-start | bytes 1572868
  0.7 29.3 %copy-start.8 = (bf16[512,512]{1,0:T(8,128)(2,1)S(1)}, bf16[512,512]{1,0:T(8,128)(2,1)}, u32[]{:S(2)}) copy-start(bf16[512,512]{1,0:T(8,128)(2,1)} %param.11) | copy-start | bytes 1572868
  2.1 27.9 %collective-permute-start.2 = (bf16[2,512,512]{2,1,0:T(8,128)(2,1)S(1)}, bf16[2,512,512]{2,1,0:T(8,128)(2,1)}, u32[]{:S(2)}, u32[]{:S(2)}) collective-permute-start(bf16[2,512,512]{2,1,0:T(8,128)(2,1)S(1)} %pad_maximum_fusion.3), channel_id=1, source_target_pairs={{0,2},{1,3},{2,0},{3,1},{4,6},{5,7},{6,4},{7,5},{8,10},{9,11},{10,... | collective-permute-start | bytes 3145736 | tf_op jit(solution)/shard_map/ppermute | solution.py:31
  5.1 31.5 %collective-permute-start = (bf16[1,32,3,512]{3,2,1,0:T(4,128)(2,1)}, bf16[1,32,3,512]{3,2,1,0:T(4,128)(2,1)S(1)}, u32[]{:S(2)}, u32[]{:S(2)}) collective-permute-start(bf16[1,32,3,512]{3,2,1,0:T(4,128)(2,1)} %get-tuple-element.130), channel_id=1, source_target_pairs={{0,4},{4,8},{8,12},{12,16},{16,20},{20,24},{24,28},{28,32},{32,36}... | collective-permute-start | bytes 294920 | tf_op jit(solution)/shard_map/ppermute | solution.py:20
  5.1 31.7 %collective-permute-start.1 = (bf16[1,32,3,512]{3,2,1,0:T(4,128)(2,1)S(1)}, bf16[1,32,3,512]{3,2,1,0:T(4,128)(2,1)S(1)}, u32[]{:S(2)}, u32[]{:S(2)}) collective-permute-start(bf16[1,32,3,512]{3,2,1,0:T(4,128)(2,1)S(1)} %get-tuple-element.131), channel_id=1, source_target_pairs={{4,0},{8,4},{12,8},{16,12},{20,16},{24,20},{28,24},{32,28},{36,32}... | collective-permute-start | bytes 294920 | tf_op jit(solution)/shard_map/ppermute | solution.py:22
  31.4 1.7 copy-start.115
  32.9 13.7 %collective-permute-start.3 = (bf16[2,2,512,512]{3,2,1,0:T(8,128)(2,1)}, bf16[2,2,512,512]{3,2,1,0:T(8,128)(2,1)}, u32[]{:S(2)}, u32[]{:S(2)}) collective-permute-start(bf16[2,2,512,512]{3,2,1,0:T(8,128)(2,1)} %pad_maximum_fusion.2), channel_id=1, source_target_pairs={{0,1},{1,0},{2,3},{3,2},{4,5},{5,4},{6,7},{7,6},{8,9},{9,8},{10,11... | collective-permute-start | bytes 6291464 | tf_op jit(solution)/shard_map/ppermute | solution.py:31
  36.9 1.6 copy-start.5
  36.9 1.6 copy-start.15
  36.9 1.6 copy-start.16
  36.9 1.6 copy-start.17
  36.9 1.6 copy-start.18
  36.9 1.6 copy-start.19
  37.0 1.6 copy-start.20
  37.0 1.6 copy-start.21
  37.0 1.6 copy-start.22
  51.4 2.8 %copy-start.111 = (f32[512]{0:T(512)S(1)}, f32[512]{0:T(512)}, u32[]{:S(2)}) copy-start(f32[512]{0:T(512)} %param.10) | copy-start | bytes 6148
  54.2 3.0 %copy-start.9 = (bf16[4,1,512,512]{3,2,1,0:T(8,128)(2,1)S(1)}, bf16[4,1,512,512]{3,2,1,0:T(8,128)(2,1)}, u32[]{:S(2)}) copy-start(bf16[4,1,512,512]{3,2,1,0:T(8,128)(2,1)} %get-tuple-element.63) | copy-start | bytes 6291460
  54.2 3.0 %copy-start.12 = (bf16[1,32,8,512]{3,2,1,0:T(8,128)(2,1)S(1)}, bf16[1,32,8,512]{3,2,1,0:T(8,128)(2,1)}, u32[]{:S(2)}) copy-start(bf16[1,32,8,512]{3,2,1,0:T(8,128)(2,1)} %param.13) | copy-start | bytes 786436
  61.8 2.3 %copy-start.1 = (f32[1,32,8,512]{3,2,1,0:T(8,128)S(1)}, f32[1,32,8,512]{3,2,1,0:T(8,128)}, u32[]{:S(2)}) copy-start(f32[1,32,8,512]{3,2,1,0:T(8,128)} %get-tuple-element.62) | copy-start | bytes 1572868
  69.5 1.8 copy-start.2
  69.5 1.8 copy-start.11
  76.8 2.8 %copy-start = (bf16[2,2,1088,512]{3,2,1,0:T(8,128)(2,1)}, bf16[2,2,1088,512]{3,2,1,0:T(8,128)(2,1)S(1)}, u32[]{:S(2)}) copy-start(bf16[2,2,1088,512]{3,2,1,0:T(8,128)(2,1)S(1)} %copy.25) | copy-start | bytes 13369348
  76.9 4.5 %copy-start.56 = (f32[1,512]{1,0:T(1,128)S(1)}, f32[1,512]{1,0:T(1,128)}, u32[]{:S(2)}) copy-start(f32[1,512]{1,0:T(1,128)} %get-tuple-element.136) | copy-start | bytes 6148
  76.9 4.5 %copy-start.58 = (f32[1,512]{1,0:T(1,128)S(1)}, f32[1,512]{1,0:T(1,128)}, u32[]{:S(2)}) copy-start(f32[1,512]{1,0:T(1,128)} %get-tuple-element.137) | copy-start | bytes 6148
  76.9 4.5 %copy-start.60 = (f32[1,512]{1,0:T(1,128)S(1)}, f32[1,512]{1,0:T(1,128)}, u32[]{:S(2)}) copy-start(f32[1,512]{1,0:T(1,128)} %get-tuple-element.138) | copy-start | bytes 6148
  76.9 4.5 %copy-start.62 = (f32[1,512]{1,0:T(1,128)S(1)}, f32[1,512]{1,0:T(1,128)}, u32[]{:S(2)}) copy-start(f32[1,512]{1,0:T(1,128)} %get-tuple-element.139) | copy-start | bytes 6148
  76.9 4.5 %copy-start.64 = (f32[1,512]{1,0:T(1,128)S(1)}, f32[1,512]{1,0:T(1,128)}, u32[]{:S(2)}) copy-start(f32[1,512]{1,0:T(1,128)} %get-tuple-element.140) | copy-start | bytes 6148
  76.9 4.5 %copy-start.66 = (f32[1,512]{1,0:T(1,128)S(1)}, f32[1,512]{1,0:T(1,128)}, u32[]{:S(2)}) copy-start(f32[1,512]{1,0:T(1,128)} %get-tuple-element.141) | copy-start | bytes 6148
  76.9 4.5 %copy-start.68 = (f32[1,512]{1,0:T(1,128)S(1)}, f32[1,512]{1,0:T(1,128)}, u32[]{:S(2)}) copy-start(f32[1,512]{1,0:T(1,128)} %get-tuple-element.142) | copy-start | bytes 6148
  76.9 4.5 %copy-start.69 = (f32[1,512]{1,0:T(1,128)S(1)}, f32[1,512]{1,0:T(1,128)}, u32[]{:S(2)}) copy-start(f32[1,512]{1,0:T(1,128)} %get-tuple-element.143) | copy-start | bytes 6148
  76.9 4.5 %copy-start.70 = (f32[1,512]{1,0:T(1,128)S(1)}, f32[1,512]{1,0:T(1,128)}, u32[]{:S(2)}) copy-start(f32[1,512]{1,0:T(1,128)} %get-tuple-element.144) | copy-start | bytes 6148
  76.9 4.5 %copy-start.71 = (f32[1,512]{1,0:T(1,128)S(1)}, f32[1,512]{1,0:T(1,128)}, u32[]{:S(2)}) copy-start(f32[1,512]{1,0:T(1,128)} %get-tuple-element.145) | copy-start | bytes 6148
  77.0 4.5 %copy-start.72 = (f32[1,512]{1,0:T(1,128)S(1)}, f32[1,512]{1,0:T(1,128)}, u32[]{:S(2)}) copy-start(f32[1,512]{1,0:T(1,128)} %get-tuple-element.146) | copy-start | bytes 6148
  77.0 4.5 %copy-start.73 = (f32[1,512]{1,0:T(1,128)S(1)}, f32[1,512]{1,0:T(1,128)}, u32[]{:S(2)}) copy-start(f32[1,512]{1,0:T(1,128)} %get-tuple-element.147) | copy-start | bytes 6148
  77.0 4.5 %copy-start.74 = (f32[1,512]{1,0:T(1,128)S(1)}, f32[1,512]{1,0:T(1,128)}, u32[]{:S(2)}) copy-start(f32[1,512]{1,0:T(1,128)} %get-tuple-element.148) | copy-start | bytes 6148
  79.7 5.6 %collective-permute-start.6 = (bf16[2176,512]{1,0:T(8,128)(2,1)}, bf16[2176,512]{1,0:T(8,128)(2,1)}, u32[]{:S(2)}, u32[]{:S(2)}) collective-permute-start(bf16[2176,512]{1,0:T(8,128)(2,1)} %constant_dynamic-slice_fusion), channel_id=1, source_target_pairs={{0,1},{1,0},{2,3},{3,2},{4,5},{5,4},{6,7},{7,6},{8,9},{9,8},{10,11... | collective-permute-start | bytes 6684680 | tf_op jit(solution)/shard_map/ppermute | solution.py:31
  82.6 2.7 %slice-start = ((s8[4456448]{0:T(1024)(128)(4,1)}), s8[4194304]{0:T(1024)(128)(4,1)S(1)}, s32[]{:S(2)}) async-start(s8[4456448]{0:T(1024)(128)(4,1)} %bitcast.286), calls=%async_computation | async-start | bytes 8388608
  87.6 26.6 %collective-permute-start.7 = (bf16[1088,512]{1,0:T(8,128)(2,1)S(1)}, bf16[1088,512]{1,0:T(8,128)(2,1)S(1)}, u32[]{:S(2)}, u32[]{:S(2)}) collective-permute-start(bf16[1088,512]{1,0:T(8,128)(2,1)S(1)} %dynamic-slice_convert_fusion), channel_id=1, source_target_pairs={{0,2},{1,3},{2,0},{3,1},{4,6},{5,7},{6,4},{7,5},{8,10},{9,11},{10,... | collective-permute-start | bytes 3342344 | tf_op jit(solution)/shard_map/ppermute | solution.py:31
  114.2 4.1 %copy-start.10 = (bf16[4,1,512,512]{3,2,1,0:T(8,128)(2,1)S(1)}, bf16[4,1,512,512]{3,2,1,0:T(8,128)(2,1)}, u32[]{:S(2)}) copy-start(bf16[4,1,512,512]{3,2,1,0:T(8,128)(2,1)} %get-tuple-element.63) | copy-start | bytes 6291460
  114.5 3.7 %copy-start.3 = (bf16[256,2048]{1,0:T(8,128)(2,1)S(1)}, bf16[256,2048]{1,0:T(8,128)(2,1)}, u32[]{:S(2)}) copy-start(bf16[256,2048]{1,0:T(8,128)(2,1)} %get-tuple-element.186) | copy-start | bytes 3145732
  114.6 3.7 %copy-start.6 = (bf16[1,32,8,512]{3,2,1,0:T(8,128)(2,1)S(1)}, bf16[1,32,8,512]{3,2,1,0:T(8,128)(2,1)}, u32[]{:S(2)}) copy-start(bf16[1,32,8,512]{3,2,1,0:T(8,128)(2,1)} %param.7) | copy-start | bytes 786436
  114.7 11.1 %collective-permute-start.8 = (bf16[272,512]{1,0:T(8,128)(2,1)S(1)}, bf16[272,512]{1,0:T(8,128)(2,1)S(1)}, u32[]{:S(2)}, u32[]{:S(2)}) collective-permute-start(bf16[272,512]{1,0:T(8,128)(2,1)S(1)} %get-tuple-element.67), channel_id=1, source_target_pairs={{0,8},{4,12},{8,0},{12,4},{16,24},{20,28},{24,16},{28,20},{32,40},... | collective-permute-start | bytes 835592 | tf_op jit(solution)/shard_map/ppermute | solution.py:78
  115.0 14.8 %collective-permute-start.10 = (bf16[272,512]{1,0:T(8,128)(2,1)S(1)}, bf16[272,512]{1,0:T(8,128)(2,1)S(1)}, u32[]{:S(2)}, u32[]{:S(2)}) collective-permute-start(bf16[272,512]{1,0:T(8,128)(2,1)S(1)} %get-tuple-element.68), channel_id=1, source_target_pairs={{0,12},{4,8},{8,4},{12,0},{16,28},{20,24},{24,20},{28,16},{32,44},... | collective-permute-start | bytes 835592 | tf_op jit(solution)/shard_map/ppermute | solution.py:78
  116.1 13.7 %collective-permute-start.9 = (bf16[272,512]{1,0:T(8,128)(2,1)S(1)}, bf16[272,512]{1,0:T(8,128)(2,1)S(1)}, u32[]{:S(2)}, u32[]{:S(2)}) collective-permute-start(bf16[272,512]{1,0:T(8,128)(2,1)S(1)} %get-tuple-element.69), channel_id=1, source_target_pairs={{0,4},{4,0},{8,12},{12,8},{16,20},{20,16},{24,28},{28,24},{32,36},... | collective-permute-start | bytes 835592 | tf_op jit(solution)/shard_map/ppermute | solution.py:78
  130.0 8.0 %collective-permute-start.11 = (bf16[68,512]{1,0:T(8,128)(2,1)S(1)}, bf16[68,512]{1,0:T(8,128)(2,1)S(1)}, u32[]{:S(2)}, u32[]{:S(2)}) collective-permute-start(bf16[68,512]{1,0:T(8,128)(2,1)S(1)} %get-tuple-element.78), channel_id=1, source_target_pairs={{0,32},{4,36},{8,40},{12,44},{16,48},{20,52},{24,56},{28,60},{32,0... | collective-permute-start | bytes 208904 | tf_op jit(solution)/shard_map/ppermute | solution.py:78
  131.2 6.9 %collective-permute-start.13 = (bf16[68,512]{1,0:T(8,128)(2,1)S(1)}, bf16[68,512]{1,0:T(8,128)(2,1)S(1)}, u32[]{:S(2)}, u32[]{:S(2)}) collective-permute-start(bf16[68,512]{1,0:T(8,128)(2,1)S(1)} %get-tuple-element.79), channel_id=1, source_target_pairs={{0,48},{4,52},{8,56},{12,60},{16,32},{20,36},{24,40},{28,44},{32,1... | collective-permute-start | bytes 208904 | tf_op jit(solution)/shard_map/ppermute | solution.py:78
  132.6 6.7 %collective-permute-start.12 = (bf16[68,512]{1,0:T(8,128)(2,1)S(1)}, bf16[68,512]{1,0:T(8,128)(2,1)S(1)}, u32[]{:S(2)}, u32[]{:S(2)}) collective-permute-start(bf16[68,512]{1,0:T(8,128)(2,1)S(1)} %get-tuple-element.80), channel_id=1, source_target_pairs={{0,16},{4,20},{8,24},{12,28},{16,0},{20,4},{24,8},{28,12},{32,48},... | collective-permute-start | bytes 208904 | tf_op jit(solution)/shard_map/ppermute | solution.py:78
  139.4 9.1 %collective-permute-start.14 = (bf16[17,512]{1,0:T(8,128)(2,1)S(1)}, bf16[17,512]{1,0:T(8,128)(2,1)S(1)}, u32[]{:S(2)}, u32[]{:S(2)}) collective-permute-start(bf16[17,512]{1,0:T(8,128)(2,1)S(1)} %get-tuple-element.132), channel_id=1, source_target_pairs={{0,128},{4,132},{8,136},{12,140},{16,144},{20,148},{24,152},{28,15... | collective-permute-start | bytes 52232 | tf_op jit(solution)/shard_map/ppermute | solution.py:78
  141.8 10.1 %collective-permute-start.16 = (bf16[17,512]{1,0:T(8,128)(2,1)S(1)}, bf16[17,512]{1,0:T(8,128)(2,1)S(1)}, u32[]{:S(2)}, u32[]{:S(2)}) collective-permute-start(bf16[17,512]{1,0:T(8,128)(2,1)S(1)} %get-tuple-element.133), channel_id=1, source_target_pairs={{0,192},{4,196},{8,200},{12,204},{16,208},{20,212},{24,216},{28,22... | collective-permute-start | bytes 52232 | tf_op jit(solution)/shard_map/ppermute | solution.py:78
  147.7 7.7 %collective-permute-start.15 = (bf16[17,512]{1,0:T(8,128)(2,1)S(1)}, bf16[17,512]{1,0:T(8,128)(2,1)S(1)}, u32[]{:S(2)}, u32[]{:S(2)}) collective-permute-start(bf16[17,512]{1,0:T(8,128)(2,1)S(1)} %get-tuple-element.134), channel_id=1, source_target_pairs={{0,64},{4,68},{8,72},{12,76},{16,80},{20,84},{24,88},{28,92},{32,9... | collective-permute-start | bytes 52232 | tf_op jit(solution)/shard_map/ppermute | solution.py:78
  155.4 14.9 %collective-permute-start.19 = (bf16[17,512]{1,0:T(8,128)(2,1)S(1)}, bf16[17,512]{1,0:T(8,128)(2,1)S(1)}, u32[]{:S(2)}, u32[]{:S(2)}) collective-permute-start(bf16[17,512]{1,0:T(8,128)(2,1)S(1)} %add_convert_fusion), channel_id=1, source_target_pairs={{0,192},{4,196},{8,200},{12,204},{16,208},{20,212},{24,216},{28,22... | collective-permute-start | bytes 52232 | tf_op jit(solution)/shard_map/ppermute | solution.py:78
  158.0 11.9 %collective-permute-start.18 = (bf16[17,512]{1,0:T(8,128)(2,1)S(1)}, bf16[17,512]{1,0:T(8,128)(2,1)S(1)}, u32[]{:S(2)}, u32[]{:S(2)}) collective-permute-start(bf16[17,512]{1,0:T(8,128)(2,1)S(1)} %add_convert_fusion), channel_id=1, source_target_pairs={{0,64},{4,68},{8,72},{12,76},{16,80},{20,84},{24,88},{28,92},{32,9... | collective-permute-start | bytes 52232 | tf_op jit(solution)/shard_map/ppermute | solution.py:78
  163.2 6.3 %collective-permute-start.17 = (bf16[17,512]{1,0:T(8,128)(2,1)S(1)}, bf16[17,512]{1,0:T(8,128)(2,1)S(1)}, u32[]{:S(2)}, u32[]{:S(2)}) collective-permute-start(bf16[17,512]{1,0:T(8,128)(2,1)S(1)} %add_convert_fusion), channel_id=1, source_target_pairs={{0,128},{4,132},{8,136},{12,140},{16,144},{20,148},{24,152},{28,15... | collective-permute-start | bytes 52232 | tf_op jit(solution)/shard_map/ppermute | solution.py:78
  164.6 16.3 %collective-permute-start.5 = (bf16[1,32,3,512]{3,2,1,0:T(4,128)(2,1)S(1)}, bf16[1,32,3,512]{3,2,1,0:T(4,128)(2,1)S(1)}, u32[]{:S(2)}, u32[]{:S(2)}) collective-permute-start(bf16[1,32,3,512]{3,2,1,0:T(4,128)(2,1)S(1)} %fusion.96), channel_id=1, source_target_pairs={{4,0},{8,4},{12,8},{16,12},{20,16},{24,20},{28,24},{32,28},{36,32}... | collective-permute-start | bytes 294920 | tf_op jit(solution)/shard_map/ppermute | solution.py:22
  169.1 11.8 %collective-permute-start.4 = (bf16[1,32,3,512]{3,2,1,0:T(4,128)(2,1)S(1)}, bf16[1,32,3,512]{3,2,1,0:T(4,128)(2,1)S(1)}, u32[]{:S(2)}, u32[]{:S(2)}) collective-permute-start(bf16[1,32,3,512]{3,2,1,0:T(4,128)(2,1)S(1)} %fusion.95), channel_id=1, source_target_pairs={{0,4},{4,8},{8,12},{12,16},{16,20},{20,24},{24,28},{28,32},{32,36}... | collective-permute-start | bytes 294920 | tf_op jit(solution)/shard_map/ppermute | solution.py:20
  170.6 8.5 %collective-permute-start.22 = (bf16[68,512]{1,0:T(8,128)(2,1)S(1)}, bf16[68,512]{1,0:T(8,128)(2,1)S(1)}, u32[]{:S(2)}, u32[]{:S(2)}) collective-permute-start(bf16[68,512]{1,0:T(8,128)(2,1)S(1)} %dynamic_update_slice.39), channel_id=1, source_target_pairs={{0,48},{4,52},{8,56},{12,60},{16,32},{20,36},{24,40},{28,44},{32,1... | collective-permute-start | bytes 208904 | tf_op jit(solution)/shard_map/ppermute | solution.py:78
  172.1 6.3 %collective-permute-start.21 = (bf16[68,512]{1,0:T(8,128)(2,1)S(1)}, bf16[68,512]{1,0:T(8,128)(2,1)S(1)}, u32[]{:S(2)}, u32[]{:S(2)}) collective-permute-start(bf16[68,512]{1,0:T(8,128)(2,1)S(1)} %dynamic_update_slice.39), channel_id=1, source_target_pairs={{0,16},{4,20},{8,24},{12,28},{16,0},{20,4},{24,8},{28,12},{32,48},... | collective-permute-start | bytes 208904 | tf_op jit(solution)/shard_map/ppermute | solution.py:78
  172.2 5.5 %collective-permute-start.20 = (bf16[68,512]{1,0:T(8,128)(2,1)S(1)}, bf16[68,512]{1,0:T(8,128)(2,1)S(1)}, u32[]{:S(2)}, u32[]{:S(2)}) collective-permute-start(bf16[68,512]{1,0:T(8,128)(2,1)S(1)} %dynamic_update_slice.39), channel_id=1, source_target_pairs={{0,32},{4,36},{8,40},{12,44},{16,48},{20,52},{24,56},{28,60},{32,0... | collective-permute-start | bytes 208904 | tf_op jit(solution)/shard_map/ppermute | solution.py:78
  179.6 11.1 %collective-permute-start.23 = (bf16[272,512]{1,0:T(8,128)(2,1)S(1)}, bf16[272,512]{1,0:T(8,128)(2,1)S(1)}, u32[]{:S(2)}, u32[]{:S(2)}) collective-permute-start(bf16[272,512]{1,0:T(8,128)(2,1)S(1)} %dynamic_update_slice.43), channel_id=1, source_target_pairs={{0,8},{4,12},{8,0},{12,4},{16,24},{20,28},{24,16},{28,20},{32,40},... | collective-permute-start | bytes 835592 | tf_op jit(solution)/shard_map/ppermute | solution.py:78
  181.2 14.3 %collective-permute-start.24 = (bf16[272,512]{1,0:T(8,128)(2,1)S(1)}, bf16[272,512]{1,0:T(8,128)(2,1)S(1)}, u32[]{:S(2)}, u32[]{:S(2)}) collective-permute-start(bf16[272,512]{1,0:T(8,128)(2,1)S(1)} %dynamic_update_slice.43), channel_id=1, source_target_pairs={{0,4},{4,0},{8,12},{12,8},{16,20},{20,16},{24,28},{28,24},{32,36},... | collective-permute-start | bytes 835592 | tf_op jit(solution)/shard_map/ppermute | solution.py:78
  186.8 8.8 %collective-permute-start.25 = (bf16[272,512]{1,0:T(8,128)(2,1)S(1)}, bf16[272,512]{1,0:T(8,128)(2,1)S(1)}, u32[]{:S(2)}, u32[]{:S(2)}) collective-permute-start(bf16[272,512]{1,0:T(8,128)(2,1)S(1)} %dynamic_update_slice.43), channel_id=1, source_target_pairs={{0,12},{4,8},{8,4},{12,0},{16,28},{20,24},{24,20},{28,16},{32,44},... | collective-permute-start | bytes 835592 | tf_op jit(solution)/shard_map/ppermute | solution.py:78
  (80 other events, 105.0 us)

commit v2 on v1

--- a/solution.py
+++ b/solution.py
@@ -46,15 +46,20 @@
 def tile_summed(chunk):
     assert lax.axis_size("tile") == 64
     me = lax.axis_index("tile")
-    groups = ((0, 1), (2, 3), (4, 5))
+    groups = ((0, 1, 5), (2, 3, 4))
 
     def masks(group):
-        mine = ((me >> group[0]) & 1) * 2 + ((me >> group[1]) & 1)
-        return mine, [(d, ((d >> 1) << group[0]) | ((d & 1) << group[1])) for d in (1, 2, 3)]
+        k = len(group)
+        mine = sum(((me >> bit) & 1) << (k - 1 - j) for j, bit in enumerate(group))
+        partners = []
+        for d in range(1, 1 << k):
+            mask = sum(((d >> (k - 1 - j)) & 1) << bit for j, bit in enumerate(group))
+            partners.append((d, mask))
+        return mine, partners
 
     for group in groups:
         mine, partners = masks(group)
-        size = chunk.shape[0] // 4
+        size = chunk.shape[0] >> len(group)
         total = lax.dynamic_slice_in_dim(chunk, mine * size, size, 0)
         for d, mask in partners:
             send = lax.dynamic_slice_in_dim(chunk, (mine ^ d) * size, size, 0)
@@ -64,7 +69,7 @@
     for group in reversed(groups):
         mine, partners = masks(group)
         size = chunk.shape[0]
-        whole = jnp.zeros((4 * size,) + chunk.shape[1:], chunk.dtype)
+        whole = jnp.zeros(((size << len(group)),) + chunk.shape[1:], chunk.dtype)
         whole = lax.dynamic_update_slice_in_dim(whole, chunk, mine * size, 0)
         for d, mask in partners:
             got = swapped(chunk, "tile", mask)

time: 202 us -> 210 us (1.040)
  the two profiles are of different devices: /device:TPU:8 before, /device:TPU:32 now
where the time goes in v2:
time: 210 us; the launch traced here: 207 us
  starting transfers between devices  74.1 us (35%)
  waiting for transfers between devices  52.2 us (25%)
  other arithmetic  37.2 us (18%)
  local copies, waits for them, and re-layouts  25 us (12%)
  matrix products  11.1 us (5%)
  between operations  7.11 us (3%)
    ppermute x28, starting transfers between devices, swapped(): return lax.ppermute(value, axis, [(i, i ^ mask) for i in range(count)])  63.9 us
    ppermute x4, waiting for transfers between devices, exchange(): return lax.ppermute(value, axis, [(i, i ^ 1 << bit) for i in range(count)])  32 us
    ppermute x28, waiting for transfers between devices, swapped(): return lax.ppermute(value, axis, [(i, i ^ mask) for i in range(count)])  20.2 us
    add_any x1, other arithmetic, depthwise(): padded[:, row:row + height, col:col + width, :] * kernel[7 * row + col]  6.76 us
    reduce_sum x1, other arithmetic, body(): mean = jnp.mean(rows, axis=-1, keepdims=True)  6.23 us
    reduce_sum x3, other arithmetic, depthwise(): padded[:, row:row + height, col:col + width, :] * kernel[7 * row + col]  5.4 us
  transfers between devices with their start and end apart: 36, of which 10 were waited for; matrix products, arithmetic and copies ran while one was open for 16% of the time, Pallas kernels for 0%

profile of v2, /device:TPU:32, one launch (start us, length us, event | category | flops | bytes accessed | tf_op | source)
XLA Modules:
  0.0 206.6 jit_solution(8845518529866248489)
XLA Ops:
  0.7 1.4 pad_maximum_fusion.3
  2.1 1.7 collective-permute-start.2
  3.7 0.7 fusion.111
  4.5 1.5 collective-permute-start
  6.0 2.6 %collective-permute-start.1 = (bf16[1,32,3,512]{3,2,1,0:T(4,128)(2,1)S(1)}, bf16[1,32,3,512]{3,2,1,0:T(4,128)(2,1)S(1)}, u32[]{:S(2)}, u32[]{:S(2)}) collective-permute-start(bf16[1,32,3,512]{3,2,1,0:T(4,128)(2,1)S(1)} %get-tuple-element.139), channel_id=1, source_target_pairs={{4,0},{8,4},{12,8},{16,12},{20,16},{24,20},{28,24},{32,28},{36,32}... | collective-permute-start | bytes 294920 | tf_op jit(solution)/shard_map/ppermute | solution.py:22
  10.6 16.6 %collective-permute-done.2 = bf16[2,512,512]{2,1,0:T(8,128)(2,1)} collective-permute-done((bf16[2,512,512]{2,1,0:T(8,128)(2,1)S(1)}, bf16[2,512,512]{2,1,0:T(8,128)(2,1)}, u32[]{:S(2)}, u32[]{:S(2)}) %collective-permute-start.2) | collective-permute-done | bytes 1048608 | tf_op jit(solution)/shard_map/ppermute | solution.py:31
  27.2 1.4 select_bitcast_fusion.3
  28.6 1.5 pad_maximum_fusion.2
  34.9 1.2 fusion.104
  36.5 6.2 %fusion.106 = (f32[32,8]{1,0:T(8,128)S(1)}, f32[1,32,8,512]{3,2,1,0:T(8,128)}) fusion(f32[512]{0:T(512)S(1)} %bitcast.317, bf16[1,38,14,512]{3,2,1,0:T(8,128)(2,1)S(1)} %get-tuple-element.60, f32[512]{0:T(512)S(1)} %bitcast.335, f32[512]{0:T(512)S(1)} %bitcast.371, f32[512]{0:T(512)S(1)} %bitcast.373, f32[512]{0:T(512)S(1)} %bitcast.375, ...), kind=kLoop, calls=%fused_computation.289 | loop fusion | flops 21626624 | bytes 12094464 | tf_op jit(solution)/shard_map/reduce_sum | solution.py:140
  42.8 1.2 multiply_reduce_fusion.2
  44.2 1.9 select_bitcast_fusion.1
  46.4 2.5 %fusion.108 = (bf16[4,1,512,512]{3,2,1,0:T(8,128)(2,1)}, bf16[512,4,512]{2,0,1:T(8,128)(2,1)}) fusion(bf16[4,2,512,512]{3,2,1,0:T(8,128)(2,1)S(1)} %bitcast.289), kind=kLoop, calls=%fused_computation.290 | loop fusion | bytes 8388608 | tf_op jit(solution)/shard_map/slice | solution.py:149
  48.9 2.8 %copy.19 = bf16[512,4,512]{0,2,1:T(8,128)(2,1)S(1)} copy(bf16[512,4,512]{2,0,1:T(8,128)(2,1)} %get-tuple-element.64) | data formatting | bytes 4194304 | tf_op jit(solution)/shard_map/transpose | solution.py:148
  51.8 3.0 %multiply_convert_fusion.2 = (bf16[256,2048]{1,0:T(8,128)(2,1)}, f32[256,2048]{1,0:T(8,128)S(1)}) fusion(bf16[512,2048]{0,1:T(8,128)(2,1)S(1)} %bitcast.290, f32[512]{0:T(512)S(1)} %copy-done.111, f32[32,8]{1,0:T(8,128)S(1)} %add_rsqrt_fusion, f32[1,32,8,512]{3,2,1,0:T(8,128)} %get-tuple-element.62, f32[32,8]{1,0:T(8,128)S(1)} %broadcast_multiply_fusion), kind=kOutput, calls=%fused_computation.17 | convolution fusion | flops 540016640 | bytes 5771264 | tf_op jit(solution)/shard_map/dot_general | solution.py:150
  54.8 2.0 fusion.1
  56.8 2.6 %reshape.1319 = bf16[256,2,2,512]{3,2,1,0:T(2,128)(2,1)} reshape(bf16[256,2048]{1,0:T(8,128)(2,1)} %fusion.1) | data formatting | bytes 2097152 | tf_op jit(solution)/shard_map/reshape | solution.py:187
  59.4 2.3 %multiply_reduce_fusion = (f32[512]{0:T(512)S(1)}, f32[256]{0:T(256)S(1)}, f32[256]{0:T(256)S(1)}, f32[256,512]{1,0:T(8,128)S(1)}) fusion(f32[1,32,8,512]{3,2,1,0:T(8,128)} %get-tuple-element.62, f32[256]{0:T(256)S(1)} %rsqrt.13, f32[256]{0:T(256)S(1)} %div.17, f32[512]{0:T(512)S(1)} %copy-done.111, bf16[256,2048]{1,0:T(8,128)(2,1)} %fusion.1, ...), kind=kOutput, calls=%fused_computation.226 | convolution fusion | flops 537918464 | bytes 4202496 | tf_op jit(solution)/shard_map/dot_general | solution.py:157
  61.7 2.3 %fusion.87 = (f32[512]{0:T(512)}, f32[512]{0:T(512)}, f32[512]{0:T(512)}, f32[512]{0:T(512)}, f32[512]{0:T(512)}, /*index=5*/f32[512]{0:T(512)}, f32[512]{0:T(51...) fusion(f32[1,38,14,512]{3,2,1,0:T(8,128)S(1)} %get-tuple-elemen, ...), kind=kLoop, calls=%fused_computation.169 | loop fusion | flops 4318720 | bytes 8421376 | tf_op jit(solution)/shard_map/transpose(jvp())/reduce_sum | solution.py:119
  64.0 1.5 fusion.88
  65.5 1.6 fusion.89
  67.1 1.8 copy.30
  69.0 1.6 fusion.5
  72.1 1.0 multiply_convert_fusion.4
  74.8 1.7 copy-done
  78.6 0.9 bitcast_multiply_fusion.46
  79.6 1.2 bitcast_multiply_fusion.47
  80.9 1.2 bitcast_multiply_fusion.48
  82.2 2.3 %convert_add_fusion = bf16[2176,512]{1,0:T(8,128)(2,1)S(1)} fusion(bf16[2176,512]{1,0:T(8,128)(2,1)} %collective-permute-done.6, bf16[4352,512]{1,0:T(8,128)(2,1)S(1)} %bitcast.288, s32[]{:T(128)S(6)} %select_n.122), kind=kLoop, calls=%fused_computation.1 | loop fusion | flops 4456448 | bytes 6684676 | tf_op jit(solution)/shard_map/add | solution.py:42
  84.5 1.7 collective-permute-start.7
  86.2 6.8 %pad_add_fusion = f32[1,38,14,512]{3,2,1,0:T(8,128)S(1)} fusion(f32[1,32,8,512]{3,2,1,0:T(8,128)S(1)} %get-tuple-element.83, f32[1,32,8,512]{3,2,1,0:T(8,128)S(1)} %get-tuple-element.84, f32[1,32,8,512]{3,2,1,0:T(8,128)S(1)} %get-tuple-element.85, f32[1,32,8,512]{3,2,1,0:T(8,128)S(1)} %get-tuple-element.86, f32[1,32,8,512]{3,2,1,0:T(8,128)S(1)} %get-tuple-element.87, ...), kind=kLoop, calls=%fused_computation.25 | loop fusion | flops 13074432 | bytes 26779648 | tf_op jit(solution)/shard_map/transpose(jvp())/add_any | solution.py:119
  93.1 1.1 copy-done.3
  94.2 1.4 fusion.9
  95.7 15.4 %collective-permute-done.7 = bf16[1088,512]{1,0:T(8,128)(2,1)S(1)} collective-permute-done((bf16[1088,512]{1,0:T(8,128)(2,1)S(1)}, bf16[1088,512]{1,0:T(8,128)(2,1)S(1)}, u32[]{:S(2)}, u32[]{:S(2)}) %collective-permute-start.7) | collective-permute-done | bytes 1114144 | tf_op jit(solution)/shard_map/ppermute | solution.py:31
  111.6 3.3 %collective-permute-start.8 = (bf16[136,512]{1,0:T(8,128)(2,1)S(1)}, bf16[136,512]{1,0:T(8,128)(2,1)S(1)}, u32[]{:S(2)}, u32[]{:S(2)}) collective-permute-start(bf16[136,512]{1,0:T(8,128)(2,1)S(1)} %get-tuple-element.67), channel_id=1, source_target_pairs={{0,128},{4,132},{8,136},{12,140},{16,144},{20,148},{24,152},{28,15... | collective-permute-start | bytes 417800 | tf_op jit(solution)/shard_map/ppermute | solution.py:83
  114.9 2.5 %collective-permute-start.14 = (bf16[136,512]{1,0:T(8,128)(2,1)S(1)}, bf16[136,512]{1,0:T(8,128)(2,1)S(1)}, u32[]{:S(2)}, u32[]{:S(2)}) collective-permute-start(bf16[136,512]{1,0:T(8,128)(2,1)S(1)} %get-tuple-element.68), channel_id=1, source_target_pairs={{0,140},{4,136},{8,132},{12,128},{16,156},{20,152},{24,148},{28,14... | collective-permute-start | bytes 417800 | tf_op jit(solution)/shard_map/ppermute | solution.py:83
  118.1 2.9 %collective-permute-start.12 = (bf16[136,512]{1,0:T(8,128)(2,1)S(1)}, bf16[136,512]{1,0:T(8,128)(2,1)S(1)}, u32[]{:S(2)}, u32[]{:S(2)}) collective-permute-start(bf16[136,512]{1,0:T(8,128)(2,1)S(1)} %get-tuple-element.70), channel_id=1, source_target_pairs={{0,132},{4,128},{8,140},{12,136},{16,148},{20,144},{24,156},{28,15... | collective-permute-start | bytes 417800 | tf_op jit(solution)/shard_map/ppermute | solution.py:83
  121.0 2.1 %collective-permute-start.11 = (bf16[136,512]{1,0:T(8,128)(2,1)S(1)}, bf16[136,512]{1,0:T(8,128)(2,1)S(1)}, u32[]{:S(2)}, u32[]{:S(2)}) collective-permute-start(bf16[136,512]{1,0:T(8,128)(2,1)S(1)} %get-tuple-element.71), channel_id=1, source_target_pairs={{0,4},{4,0},{8,12},{12,8},{16,20},{20,16},{24,28},{28,24},{32,36},... | collective-permute-start | bytes 417800 | tf_op jit(solution)/shard_map/ppermute | solution.py:83
  123.1 4.9 %collective-permute-start.10 = (bf16[136,512]{1,0:T(8,128)(2,1)S(1)}, bf16[136,512]{1,0:T(8,128)(2,1)S(1)}, u32[]{:S(2)}, u32[]{:S(2)}) collective-permute-start(bf16[136,512]{1,0:T(8,128)(2,1)S(1)} %get-tuple-element.72), channel_id=1, source_target_pairs={{0,136},{4,140},{8,128},{12,132},{16,152},{20,156},{24,144},{28,14... | collective-permute-start | bytes 417800 | tf_op jit(solution)/shard_map/ppermute | solution.py:83
  128.3 1.9 collective-permute-done.11
  130.2 3.8 %collective-permute-done.10 = bf16[136,512]{1,0:T(8,128)(2,1)S(1)} collective-permute-done((bf16[136,512]{1,0:T(8,128)(2,1)S(1)}, bf16[136,512]{1,0:T(8,128)(2,1)S(1)}, u32[]{:S(2)}, u32[]{:S(2)}) %collective-permute-start.10) | collective-permute-done | bytes 139296 | tf_op jit(solution)/shard_map/ppermute | solution.py:83
  134.1 1.8 collective-permute-done.9
  136.1 6.4 %collective-permute-start.15 = (bf16[17,512]{1,0:T(8,128)(2,1)S(1)}, bf16[17,512]{1,0:T(8,128)(2,1)S(1)}, u32[]{:S(2)}, u32[]{:S(2)}) collective-permute-start(bf16[17,512]{1,0:T(8,128)(2,1)S(1)} %get-tuple-element.131), channel_id=1, source_target_pairs={{0,64},{4,68},{8,72},{12,76},{16,80},{20,84},{24,88},{28,92},{32,9... | collective-permute-start | bytes 52232 | tf_op jit(solution)/shard_map/ppermute | solution.py:83
  142.8 1.0 collective-permute-start.20
  143.8 6.0 %collective-permute-start.19 = (bf16[17,512]{1,0:T(8,128)(2,1)S(1)}, bf16[17,512]{1,0:T(8,128)(2,1)S(1)}, u32[]{:S(2)}, u32[]{:S(2)}) collective-permute-start(bf16[17,512]{1,0:T(8,128)(2,1)S(1)} %get-tuple-element.134), channel_id=1, source_target_pairs={{0,80},{4,84},{8,88},{12,92},{16,64},{20,68},{24,72},{28,76},{32,1... | collective-permute-start | bytes 52232 | tf_op jit(solution)/shard_map/ppermute | solution.py:83
  149.8 2.4 %collective-permute-start.17 = (bf16[17,512]{1,0:T(8,128)(2,1)S(1)}, bf16[17,512]{1,0:T(8,128)(2,1)S(1)}, u32[]{:S(2)}, u32[]{:S(2)}) collective-permute-start(bf16[17,512]{1,0:T(8,128)(2,1)S(1)} %get-tuple-element.136), channel_id=1, source_target_pairs={{0,96},{4,100},{8,104},{12,108},{16,112},{20,116},{24,120},{28,124... | collective-permute-start | bytes 52232 | tf_op jit(solution)/shard_map/ppermute | solution.py:83
  152.2 2.0 collective-permute-start.16
  154.3 1.1 collective-permute-start.5
  155.4 1.0 collective-permute-start.4
  157.1 3.0 %collective-permute-start.23 = (bf16[17,512]{1,0:T(8,128)(2,1)S(1)}, bf16[17,512]{1,0:T(8,128)(2,1)S(1)}, u32[]{:S(2)}, u32[]{:S(2)}) collective-permute-start(bf16[17,512]{1,0:T(8,128)(2,1)S(1)} %add_convert_fusion), channel_id=1, source_target_pairs={{0,32},{4,36},{8,40},{12,44},{16,48},{20,52},{24,56},{28,60},{32,0... | collective-permute-start | bytes 52232 | tf_op jit(solution)/shard_map/ppermute | solution.py:83
  160.2 2.8 %collective-permute-start.22 = (bf16[17,512]{1,0:T(8,128)(2,1)S(1)}, bf16[17,512]{1,0:T(8,128)(2,1)S(1)}, u32[]{:S(2)}, u32[]{:S(2)}) collective-permute-start(bf16[17,512]{1,0:T(8,128)(2,1)S(1)} %add_convert_fusion), channel_id=1, source_target_pairs={{0,64},{4,68},{8,72},{12,76},{16,80},{20,84},{24,88},{28,92},{32,9... | collective-permute-start | bytes 52232 | tf_op jit(solution)/shard_map/ppermute | solution.py:83
  163.2 2.8 %collective-permute-start.28 = (bf16[17,512]{1,0:T(8,128)(2,1)S(1)}, bf16[17,512]{1,0:T(8,128)(2,1)S(1)}, u32[]{:S(2)}, u32[]{:S(2)}) collective-permute-start(bf16[17,512]{1,0:T(8,128)(2,1)S(1)} %add_convert_fusion), channel_id=1, source_target_pairs={{0,112},{4,116},{8,120},{12,124},{16,96},{20,100},{24,104},{28,108... | collective-permute-start | bytes 52232 | tf_op jit(solution)/shard_map/ppermute | solution.py:83
  166.0 1.0 collective-permute-start.27
  167.0 1.7 collective-permute-start.26
  168.7 2.7 %collective-permute-start.25 = (bf16[17,512]{1,0:T(8,128)(2,1)S(1)}, bf16[17,512]{1,0:T(8,128)(2,1)S(1)}, u32[]{:S(2)}, u32[]{:S(2)}) collective-permute-start(bf16[17,512]{1,0:T(8,128)(2,1)S(1)} %add_convert_fusion), channel_id=1, source_target_pairs={{0,16},{4,20},{8,24},{12,28},{16,0},{20,4},{24,8},{28,12},{32,48},... | collective-permute-start | bytes 52232 | tf_op jit(solution)/shard_map/ppermute | solution.py:83
  173.4 4.0 %collective-permute-done.24 = bf16[17,512]{1,0:T(8,128)(2,1)S(1)} collective-permute-done((bf16[17,512]{1,0:T(8,128)(2,1)S(1)}, bf16[17,512]{1,0:T(8,128)(2,1)S(1)}, u32[]{:S(2)}, u32[]{:S(2)}) %collective-permute-start.24) | collective-permute-done | bytes 17440 | tf_op jit(solution)/shard_map/ppermute | solution.py:83
  179.3 1.7 collective-permute-start.29
  181.1 0.9 pad_maximum_fusion.6
  182.0 6.3 %collective-permute-start.35 = (bf16[136,512]{1,0:T(8,128)(2,1)S(1)}, bf16[136,512]{1,0:T(8,128)(2,1)S(1)}, u32[]{:S(2)}, u32[]{:S(2)}) collective-permute-start(bf16[136,512]{1,0:T(8,128)(2,1)S(1)} %dynamic_update_slice.55), channel_id=1, source_target_pairs={{0,140},{4,136},{8,132},{12,128},{16,156},{20,152},{24,148},{28,14... | collective-permute-start | bytes 417800 | tf_op jit(solution)/shard_map/ppermute | solution.py:83
  188.3 5.6 %collective-permute-start.30 = (bf16[136,512]{1,0:T(8,128)(2,1)S(1)}, bf16[136,512]{1,0:T(8,128)(2,1)S(1)}, u32[]{:S(2)}, u32[]{:S(2)}) collective-permute-start(bf16[136,512]{1,0:T(8,128)(2,1)S(1)} %dynamic_update_slice.55), channel_id=1, source_target_pairs={{0,8},{4,12},{8,0},{12,4},{16,24},{20,28},{24,16},{28,20},{32,40},... | collective-permute-start | bytes 417800 | tf_op jit(solution)/shard_map/ppermute | solution.py:83
  194.0 1.6 collective-permute-start.31
  195.6 2.8 %collective-permute-done.30 = bf16[136,512]{1,0:T(8,128)(2,1)S(1)} collective-permute-done((bf16[136,512]{1,0:T(8,128)(2,1)S(1)}, bf16[136,512]{1,0:T(8,128)(2,1)S(1)}, u32[]{:S(2)}, u32[]{:S(2)}) %collective-permute-start.30) | collective-permute-done | bytes 139296 | tf_op jit(solution)/shard_map/ppermute | solution.py:83
  198.4 4.6 %collective-permute-done.31 = bf16[136,512]{1,0:T(8,128)(2,1)S(1)} collective-permute-done((bf16[136,512]{1,0:T(8,128)(2,1)S(1)}, bf16[136,512]{1,0:T(8,128)(2,1)S(1)}, u32[]{:S(2)}, u32[]{:S(2)}) %collective-permute-start.31) | collective-permute-done | bytes 139296 | tf_op jit(solution)/shard_map/ppermute | solution.py:83
  204.8 1.6 fusion.110
  (330 shorter events, 16.3 us)
Async XLA Ops:
  0.6 3.1 %copy-start.4 = (bf16[1,32,8,512]{3,2,1,0:T(8,128)(2,1)S(1)}, bf16[1,32,8,512]{3,2,1,0:T(8,128)(2,1)}, u32[]{:S(2)}) copy-start(bf16[1,32,8,512]{3,2,1,0:T(8,128)(2,1)} %param.7) | copy-start | bytes 786436
  0.6 8.0 %copy-start.14 = (f32[49,512]{1,0:T(8,128)S(1)}, f32[49,512]{1,0:T(8,128)}, u32[]{:S(2)}) copy-start(f32[49,512]{1,0:T(8,128)} %param.9) | copy-start | bytes 301060
  0.7 26.5 %copy-start.7 = (bf16[512,512]{1,0:T(8,128)(2,1)S(1)}, bf16[512,512]{1,0:T(8,128)(2,1)}, u32[]{:S(2)}) copy-start(bf16[512,512]{1,0:T(8,128)(2,1)} %param.12) | copy-start | bytes 1572868
  0.7 26.5 %copy-start.8 = (bf16[512,512]{1,0:T(8,128)(2,1)S(1)}, bf16[512,512]{1,0:T(8,128)(2,1)}, u32[]{:S(2)}) copy-start(bf16[512,512]{1,0:T(8,128)(2,1)} %param.11) | copy-start | bytes 1572868
  2.1 25.1 %collective-permute-start.2 = (bf16[2,512,512]{2,1,0:T(8,128)(2,1)S(1)}, bf16[2,512,512]{2,1,0:T(8,128)(2,1)}, u32[]{:S(2)}, u32[]{:S(2)}) collective-permute-start(bf16[2,512,512]{2,1,0:T(8,128)(2,1)S(1)} %pad_maximum_fusion.3), channel_id=1, source_target_pairs={{0,2},{1,3},{2,0},{3,1},{4,6},{5,7},{6,4},{7,5},{8,10},{9,11},{10,... | collective-permute-start | bytes 3145736 | tf_op jit(solution)/shard_map/ppermute | solution.py:31
  4.5 29.7 %collective-permute-start = (bf16[1,32,3,512]{3,2,1,0:T(4,128)(2,1)}, bf16[1,32,3,512]{3,2,1,0:T(4,128)(2,1)S(1)}, u32[]{:S(2)}, u32[]{:S(2)}) collective-permute-start(bf16[1,32,3,512]{3,2,1,0:T(4,128)(2,1)} %get-tuple-element.138), channel_id=1, source_target_pairs={{0,4},{4,8},{8,12},{12,16},{16,20},{20,24},{24,28},{28,32},{32,36}... | collective-permute-start | bytes 294920 | tf_op jit(solution)/shard_map/ppermute | solution.py:20
  6.0 28.3 %collective-permute-start.1 = (bf16[1,32,3,512]{3,2,1,0:T(4,128)(2,1)S(1)}, bf16[1,32,3,512]{3,2,1,0:T(4,128)(2,1)S(1)}, u32[]{:S(2)}, u32[]{:S(2)}) collective-permute-start(bf16[1,32,3,512]{3,2,1,0:T(4,128)(2,1)S(1)} %get-tuple-element.139), channel_id=1, source_target_pairs={{4,0},{8,4},{12,8},{16,12},{20,16},{24,20},{28,24},{32,28},{36,32}... | collective-permute-start | bytes 294920 | tf_op jit(solution)/shard_map/ppermute | solution.py:22
  28.5 1.7 copy-start.115
  30.1 14.1 %collective-permute-start.3 = (bf16[2,2,512,512]{3,2,1,0:T(8,128)(2,1)}, bf16[2,2,512,512]{3,2,1,0:T(8,128)(2,1)}, u32[]{:S(2)}, u32[]{:S(2)}) collective-permute-start(bf16[2,2,512,512]{3,2,1,0:T(8,128)(2,1)} %pad_maximum_fusion.2), channel_id=1, source_target_pairs={{0,1},{1,0},{2,3},{3,2},{4,5},{5,4},{6,7},{7,6},{8,9},{9,8},{10,11... | collective-permute-start | bytes 6291464 | tf_op jit(solution)/shard_map/ppermute | solution.py:31
  34.4 1.6 copy-start.5
  48.9 2.8 %copy-start.111 = (f32[512]{0:T(512)S(1)}, f32[512]{0:T(512)}, u32[]{:S(2)}) copy-start(f32[512]{0:T(512)} %param.10) | copy-start | bytes 6148
  51.8 3.0 %copy-start.9 = (bf16[4,1,512,512]{3,2,1,0:T(8,128)(2,1)S(1)}, bf16[4,1,512,512]{3,2,1,0:T(8,128)(2,1)}, u32[]{:S(2)}) copy-start(bf16[4,1,512,512]{3,2,1,0:T(8,128)(2,1)} %get-tuple-element.63) | copy-start | bytes 6291460
  51.8 3.0 %copy-start.12 = (bf16[1,32,8,512]{3,2,1,0:T(8,128)(2,1)S(1)}, bf16[1,32,8,512]{3,2,1,0:T(8,128)(2,1)}, u32[]{:S(2)}) copy-start(bf16[1,32,8,512]{3,2,1,0:T(8,128)(2,1)} %param.13) | copy-start | bytes 786436
  59.4 2.3 %copy-start.1 = (f32[1,32,8,512]{3,2,1,0:T(8,128)S(1)}, f32[1,32,8,512]{3,2,1,0:T(8,128)}, u32[]{:S(2)}) copy-start(f32[1,32,8,512]{3,2,1,0:T(8,128)} %get-tuple-element.62) | copy-start | bytes 1572868
  67.1 1.8 copy-start.2
  67.1 1.8 copy-start.11
  74.5 2.0 copy-start
  74.5 3.9 %copy-start.56 = (f32[1,512]{1,0:T(1,128)S(1)}, f32[1,512]{1,0:T(1,128)}, u32[]{:S(2)}) copy-start(f32[1,512]{1,0:T(1,128)} %get-tuple-element.141) | copy-start | bytes 6148
  74.5 3.9 %copy-start.58 = (f32[1,512]{1,0:T(1,128)S(1)}, f32[1,512]{1,0:T(1,128)}, u32[]{:S(2)}) copy-start(f32[1,512]{1,0:T(1,128)} %get-tuple-element.142) | copy-start | bytes 6148
  74.5 3.9 %copy-start.60 = (f32[1,512]{1,0:T(1,128)S(1)}, f32[1,512]{1,0:T(1,128)}, u32[]{:S(2)}) copy-start(f32[1,512]{1,0:T(1,128)} %get-tuple-element.143) | copy-start | bytes 6148
  74.6 3.9 %copy-start.62 = (f32[1,512]{1,0:T(1,128)S(1)}, f32[1,512]{1,0:T(1,128)}, u32[]{:S(2)}) copy-start(f32[1,512]{1,0:T(1,128)} %get-tuple-element.144) | copy-start | bytes 6148
  74.6 3.9 %copy-start.64 = (f32[1,512]{1,0:T(1,128)S(1)}, f32[1,512]{1,0:T(1,128)}, u32[]{:S(2)}) copy-start(f32[1,512]{1,0:T(1,128)} %get-tuple-element.145) | copy-start | bytes 6148
  74.6 3.9 %copy-start.66 = (f32[1,512]{1,0:T(1,128)S(1)}, f32[1,512]{1,0:T(1,128)}, u32[]{:S(2)}) copy-start(f32[1,512]{1,0:T(1,128)} %get-tuple-element.146) | copy-start | bytes 6148
  74.6 3.9 %copy-start.68 = (f32[1,512]{1,0:T(1,128)S(1)}, f32[1,512]{1,0:T(1,128)}, u32[]{:S(2)}) copy-start(f32[1,512]{1,0:T(1,128)} %get-tuple-element.147) | copy-start | bytes 6148
  74.6 3.9 %copy-start.69 = (f32[1,512]{1,0:T(1,128)S(1)}, f32[1,512]{1,0:T(1,128)}, u32[]{:S(2)}) copy-start(f32[1,512]{1,0:T(1,128)} %get-tuple-element.148) | copy-start | bytes 6148
  74.6 3.9 %copy-start.70 = (f32[1,512]{1,0:T(1,128)S(1)}, f32[1,512]{1,0:T(1,128)}, u32[]{:S(2)}) copy-start(f32[1,512]{1,0:T(1,128)} %get-tuple-element.149) | copy-start | bytes 6148
  74.6 3.9 %copy-start.71 = (f32[1,512]{1,0:T(1,128)S(1)}, f32[1,512]{1,0:T(1,128)}, u32[]{:S(2)}) copy-start(f32[1,512]{1,0:T(1,128)} %get-tuple-element.150) | copy-start | bytes 6148
  74.6 3.9 %copy-start.72 = (f32[1,512]{1,0:T(1,128)S(1)}, f32[1,512]{1,0:T(1,128)}, u32[]{:S(2)}) copy-start(f32[1,512]{1,0:T(1,128)} %get-tuple-element.151) | copy-start | bytes 6148
  74.6 3.9 %copy-start.73 = (f32[1,512]{1,0:T(1,128)S(1)}, f32[1,512]{1,0:T(1,128)}, u32[]{:S(2)}) copy-start(f32[1,512]{1,0:T(1,128)} %get-tuple-element.152) | copy-start | bytes 6148
  74.6 3.9 %copy-start.74 = (f32[1,512]{1,0:T(1,128)S(1)}, f32[1,512]{1,0:T(1,128)}, u32[]{:S(2)}) copy-start(f32[1,512]{1,0:T(1,128)} %get-tuple-element.153) | copy-start | bytes 6148
  76.6 5.6 %collective-permute-start.6 = (bf16[2176,512]{1,0:T(8,128)(2,1)S(1)}, bf16[2176,512]{1,0:T(8,128)(2,1)}, u32[]{:S(2)}, u32[]{:S(2)}) collective-permute-start(bf16[2176,512]{1,0:T(8,128)(2,1)S(1)} %constant_dynamic-slice_fusion), channel_id=1, source_target_pairs={{0,1},{1,0},{2,3},{3,2},{4,5},{5,4},{6,7},{7,6},{8,9},{9,8},{10,11... | collective-permute-start | bytes 6684680 | tf_op jit(solution)/shard_map/ppermute | solution.py:31
  79.6 2.5 %slice-start = ((s8[4456448]{0:T(1024)(128)(4,1)}), s8[4194304]{0:T(1024)(128)(4,1)S(1)}, s32[]{:S(2)}) async-start(s8[4456448]{0:T(1024)(128)(4,1)} %bitcast.286), calls=%async_computation | async-start | bytes 8388608
  84.5 26.6 %collective-permute-start.7 = (bf16[1088,512]{1,0:T(8,128)(2,1)S(1)}, bf16[1088,512]{1,0:T(8,128)(2,1)S(1)}, u32[]{:S(2)}, u32[]{:S(2)}) collective-permute-start(bf16[1088,512]{1,0:T(8,128)(2,1)S(1)} %dynamic-slice_convert_fusion), channel_id=1, source_target_pairs={{0,2},{1,3},{2,0},{3,1},{4,6},{5,7},{6,4},{7,5},{8,10},{9,11},{10,... | collective-permute-start | bytes 3342344 | tf_op jit(solution)/shard_map/ppermute | solution.py:31
  86.2 6.9 %copy-start.10 = (bf16[4,1,512,512]{3,2,1,0:T(8,128)(2,1)S(1)}, bf16[4,1,512,512]{3,2,1,0:T(8,128)(2,1)}, u32[]{:S(2)}) copy-start(bf16[4,1,512,512]{3,2,1,0:T(8,128)(2,1)} %get-tuple-element.63) | copy-start | bytes 6291460
  111.6 11.5 %collective-permute-start.8 = (bf16[136,512]{1,0:T(8,128)(2,1)S(1)}, bf16[136,512]{1,0:T(8,128)(2,1)S(1)}, u32[]{:S(2)}, u32[]{:S(2)}) collective-permute-start(bf16[136,512]{1,0:T(8,128)(2,1)S(1)} %get-tuple-element.67), channel_id=1, source_target_pairs={{0,128},{4,132},{8,136},{12,140},{16,144},{20,148},{24,152},{28,15... | collective-permute-start | bytes 417800 | tf_op jit(solution)/shard_map/ppermute | solution.py:83
  114.9 13.2 %collective-permute-start.14 = (bf16[136,512]{1,0:T(8,128)(2,1)S(1)}, bf16[136,512]{1,0:T(8,128)(2,1)S(1)}, u32[]{:S(2)}, u32[]{:S(2)}) collective-permute-start(bf16[136,512]{1,0:T(8,128)(2,1)S(1)} %get-tuple-element.68), channel_id=1, source_target_pairs={{0,140},{4,136},{8,132},{12,128},{16,156},{20,152},{24,148},{28,14... | collective-permute-start | bytes 417800 | tf_op jit(solution)/shard_map/ppermute | solution.py:83
  117.5 10.8 %collective-permute-start.13 = (bf16[136,512]{1,0:T(8,128)(2,1)S(1)}, bf16[136,512]{1,0:T(8,128)(2,1)S(1)}, u32[]{:S(2)}, u32[]{:S(2)}) collective-permute-start(bf16[136,512]{1,0:T(8,128)(2,1)S(1)} %get-tuple-element.69), channel_id=1, source_target_pairs={{0,12},{4,8},{8,4},{12,0},{16,28},{20,24},{24,20},{28,16},{32,44},... | collective-permute-start | bytes 417800 | tf_op jit(solution)/shard_map/ppermute | solution.py:83
  118.1 10.3 %collective-permute-start.12 = (bf16[136,512]{1,0:T(8,128)(2,1)S(1)}, bf16[136,512]{1,0:T(8,128)(2,1)S(1)}, u32[]{:S(2)}, u32[]{:S(2)}) collective-permute-start(bf16[136,512]{1,0:T(8,128)(2,1)S(1)} %get-tuple-element.70), channel_id=1, source_target_pairs={{0,132},{4,128},{8,140},{12,136},{16,148},{20,144},{24,156},{28,15... | collective-permute-start | bytes 417800 | tf_op jit(solution)/shard_map/ppermute | solution.py:83
  121.0 9.2 %collective-permute-start.11 = (bf16[136,512]{1,0:T(8,128)(2,1)S(1)}, bf16[136,512]{1,0:T(8,128)(2,1)S(1)}, u32[]{:S(2)}, u32[]{:S(2)}) collective-permute-start(bf16[136,512]{1,0:T(8,128)(2,1)S(1)} %get-tuple-element.71), channel_id=1, source_target_pairs={{0,4},{4,0},{8,12},{12,8},{16,20},{20,16},{24,28},{28,24},{32,36},... | collective-permute-start | bytes 417800 | tf_op jit(solution)/shard_map/ppermute | solution.py:83
  123.1 11.0 %collective-permute-start.10 = (bf16[136,512]{1,0:T(8,128)(2,1)S(1)}, bf16[136,512]{1,0:T(8,128)(2,1)S(1)}, u32[]{:S(2)}, u32[]{:S(2)}) collective-permute-start(bf16[136,512]{1,0:T(8,128)(2,1)S(1)} %get-tuple-element.72), channel_id=1, source_target_pairs={{0,136},{4,140},{8,128},{12,132},{16,152},{20,156},{24,144},{28,14... | collective-permute-start | bytes 417800 | tf_op jit(solution)/shard_map/ppermute | solution.py:83
  128.0 7.9 %collective-permute-start.9 = (bf16[136,512]{1,0:T(8,128)(2,1)S(1)}, bf16[136,512]{1,0:T(8,128)(2,1)S(1)}, u32[]{:S(2)}, u32[]{:S(2)}) collective-permute-start(bf16[136,512]{1,0:T(8,128)(2,1)S(1)} %get-tuple-element.73), channel_id=1, source_target_pairs={{0,8},{4,12},{8,0},{12,4},{16,24},{20,28},{24,16},{28,20},{32,40},... | collective-permute-start | bytes 417800 | tf_op jit(solution)/shard_map/ppermute | solution.py:83
  136.1 13.7 %collective-permute-start.15 = (bf16[17,512]{1,0:T(8,128)(2,1)S(1)}, bf16[17,512]{1,0:T(8,128)(2,1)S(1)}, u32[]{:S(2)}, u32[]{:S(2)}) collective-permute-start(bf16[17,512]{1,0:T(8,128)(2,1)S(1)} %get-tuple-element.131), channel_id=1, source_target_pairs={{0,64},{4,68},{8,72},{12,76},{16,80},{20,84},{24,88},{28,92},{32,9... | collective-permute-start | bytes 52232 | tf_op jit(solution)/shard_map/ppermute | solution.py:83
  142.5 9.7 %collective-permute-start.21 = (bf16[17,512]{1,0:T(8,128)(2,1)S(1)}, bf16[17,512]{1,0:T(8,128)(2,1)S(1)}, u32[]{:S(2)}, u32[]{:S(2)}) collective-permute-start(bf16[17,512]{1,0:T(8,128)(2,1)S(1)} %get-tuple-element.132), channel_id=1, source_target_pairs={{0,112},{4,116},{8,120},{12,124},{16,96},{20,100},{24,104},{28,108... | collective-permute-start | bytes 52232 | tf_op jit(solution)/shard_map/ppermute | solution.py:83
  142.8 11.6 %collective-permute-start.20 = (bf16[17,512]{1,0:T(8,128)(2,1)S(1)}, bf16[17,512]{1,0:T(8,128)(2,1)S(1)}, u32[]{:S(2)}, u32[]{:S(2)}) collective-permute-start(bf16[17,512]{1,0:T(8,128)(2,1)S(1)} %get-tuple-element.133), channel_id=1, source_target_pairs={{0,48},{4,52},{8,56},{12,60},{16,32},{20,36},{24,40},{28,44},{32,1... | collective-permute-start | bytes 52232 | tf_op jit(solution)/shard_map/ppermute | solution.py:83
  143.8 11.7 %collective-permute-start.19 = (bf16[17,512]{1,0:T(8,128)(2,1)S(1)}, bf16[17,512]{1,0:T(8,128)(2,1)S(1)}, u32[]{:S(2)}, u32[]{:S(2)}) collective-permute-start(bf16[17,512]{1,0:T(8,128)(2,1)S(1)} %get-tuple-element.134), channel_id=1, source_target_pairs={{0,80},{4,84},{8,88},{12,92},{16,64},{20,68},{24,72},{28,76},{32,1... | collective-permute-start | bytes 52232 | tf_op jit(solution)/shard_map/ppermute | solution.py:83
  149.8 6.6 %collective-permute-start.18 = (bf16[17,512]{1,0:T(8,128)(2,1)S(1)}, bf16[17,512]{1,0:T(8,128)(2,1)S(1)}, u32[]{:S(2)}, u32[]{:S(2)}) collective-permute-start(bf16[17,512]{1,0:T(8,128)(2,1)S(1)} %get-tuple-element.135), channel_id=1, source_target_pairs={{0,16},{4,20},{8,24},{12,28},{16,0},{20,4},{24,8},{28,12},{32,48},... | collective-permute-start | bytes 52232 | tf_op jit(solution)/shard_map/ppermute | solution.py:83
  149.8 6.6 %collective-permute-start.17 = (bf16[17,512]{1,0:T(8,128)(2,1)S(1)}, bf16[17,512]{1,0:T(8,128)(2,1)S(1)}, u32[]{:S(2)}, u32[]{:S(2)}) collective-permute-start(bf16[17,512]{1,0:T(8,128)(2,1)S(1)} %get-tuple-element.136), channel_id=1, source_target_pairs={{0,96},{4,100},{8,104},{12,108},{16,112},{20,116},{24,120},{28,124... | collective-permute-start | bytes 52232 | tf_op jit(solution)/shard_map/ppermute | solution.py:83
  152.2 4.9 %collective-permute-start.16 = (bf16[17,512]{1,0:T(8,128)(2,1)S(1)}, bf16[17,512]{1,0:T(8,128)(2,1)S(1)}, u32[]{:S(2)}, u32[]{:S(2)}) collective-permute-start(bf16[17,512]{1,0:T(8,128)(2,1)S(1)} %get-tuple-element.137), channel_id=1, source_target_pairs={{0,32},{4,36},{8,40},{12,44},{16,48},{20,52},{24,56},{28,60},{32,0... | collective-permute-start | bytes 52232 | tf_op jit(solution)/shard_map/ppermute | solution.py:83
  154.3 11.7 %collective-permute-start.5 = (bf16[1,32,3,512]{3,2,1,0:T(4,128)(2,1)S(1)}, bf16[1,32,3,512]{3,2,1,0:T(4,128)(2,1)S(1)}, u32[]{:S(2)}, u32[]{:S(2)}) collective-permute-start(bf16[1,32,3,512]{3,2,1,0:T(4,128)(2,1)S(1)} %fusion.96), channel_id=1, source_target_pairs={{4,0},{8,4},{12,8},{16,12},{20,16},{24,20},{28,24},{32,28},{36,32}... | collective-permute-start | bytes 294920 | tf_op jit(solution)/shard_map/ppermute | solution.py:22
  155.4 11.5 %collective-permute-start.4 = (bf16[1,32,3,512]{3,2,1,0:T(4,128)(2,1)S(1)}, bf16[1,32,3,512]{3,2,1,0:T(4,128)(2,1)S(1)}, u32[]{:S(2)}, u32[]{:S(2)}) collective-permute-start(bf16[1,32,3,512]{3,2,1,0:T(4,128)(2,1)S(1)} %fusion.95), channel_id=1, source_target_pairs={{0,4},{4,8},{8,12},{12,16},{16,20},{20,24},{24,28},{28,32},{32,36}... | collective-permute-start | bytes 294920 | tf_op jit(solution)/shard_map/ppermute | solution.py:20
  157.1 11.5 %collective-permute-start.23 = (bf16[17,512]{1,0:T(8,128)(2,1)S(1)}, bf16[17,512]{1,0:T(8,128)(2,1)S(1)}, u32[]{:S(2)}, u32[]{:S(2)}) collective-permute-start(bf16[17,512]{1,0:T(8,128)(2,1)S(1)} %add_convert_fusion), channel_id=1, source_target_pairs={{0,32},{4,36},{8,40},{12,44},{16,48},{20,52},{24,56},{28,60},{32,0... | collective-permute-start | bytes 52232 | tf_op jit(solution)/shard_map/ppermute | solution.py:83
  160.2 11.2 %collective-permute-start.22 = (bf16[17,512]{1,0:T(8,128)(2,1)S(1)}, bf16[17,512]{1,0:T(8,128)(2,1)S(1)}, u32[]{:S(2)}, u32[]{:S(2)}) collective-permute-start(bf16[17,512]{1,0:T(8,128)(2,1)S(1)} %add_convert_fusion), channel_id=1, source_target_pairs={{0,64},{4,68},{8,72},{12,76},{16,80},{20,84},{24,88},{28,92},{32,9... | collective-permute-start | bytes 52232 | tf_op jit(solution)/shard_map/ppermute | solution.py:83
  163.2 15.7 %collective-permute-start.28 = (bf16[17,512]{1,0:T(8,128)(2,1)S(1)}, bf16[17,512]{1,0:T(8,128)(2,1)S(1)}, u32[]{:S(2)}, u32[]{:S(2)}) collective-permute-start(bf16[17,512]{1,0:T(8,128)(2,1)S(1)} %add_convert_fusion), channel_id=1, source_target_pairs={{0,112},{4,116},{8,120},{12,124},{16,96},{20,100},{24,104},{28,108... | collective-permute-start | bytes 52232 | tf_op jit(solution)/shard_map/ppermute | solution.py:83
  166.0 12.5 %collective-permute-start.27 = (bf16[17,512]{1,0:T(8,128)(2,1)S(1)}, bf16[17,512]{1,0:T(8,128)(2,1)S(1)}, u32[]{:S(2)}, u32[]{:S(2)}) collective-permute-start(bf16[17,512]{1,0:T(8,128)(2,1)S(1)} %add_convert_fusion), channel_id=1, source_target_pairs={{0,48},{4,52},{8,56},{12,60},{16,32},{20,36},{24,40},{28,44},{32,1... | collective-permute-start | bytes 52232 | tf_op jit(solution)/shard_map/ppermute | solution.py:83
  167.0 11.1 %collective-permute-start.26 = (bf16[17,512]{1,0:T(8,128)(2,1)S(1)}, bf16[17,512]{1,0:T(8,128)(2,1)S(1)}, u32[]{:S(2)}, u32[]{:S(2)}) collective-permute-start(bf16[17,512]{1,0:T(8,128)(2,1)S(1)} %add_convert_fusion), channel_id=1, source_target_pairs={{0,80},{4,84},{8,88},{12,92},{16,64},{20,68},{24,72},{28,76},{32,1... | collective-permute-start | bytes 52232 | tf_op jit(solution)/shard_map/ppermute | solution.py:83
  168.7 9.0 %collective-permute-start.25 = (bf16[17,512]{1,0:T(8,128)(2,1)S(1)}, bf16[17,512]{1,0:T(8,128)(2,1)S(1)}, u32[]{:S(2)}, u32[]{:S(2)}) collective-permute-start(bf16[17,512]{1,0:T(8,128)(2,1)S(1)} %add_convert_fusion), channel_id=1, source_target_pairs={{0,16},{4,20},{8,24},{12,28},{16,0},{20,4},{24,8},{28,12},{32,48},... | collective-permute-start | bytes 52232 | tf_op jit(solution)/shard_map/ppermute | solution.py:83
  171.4 6.1 %collective-permute-start.24 = (bf16[17,512]{1,0:T(8,128)(2,1)S(1)}, bf16[17,512]{1,0:T(8,128)(2,1)S(1)}, u32[]{:S(2)}, u32[]{:S(2)}) collective-permute-start(bf16[17,512]{1,0:T(8,128)(2,1)S(1)} %add_convert_fusion), channel_id=1, source_target_pairs={{0,96},{4,100},{8,104},{12,108},{16,112},{20,116},{24,120},{28,124... | collective-permute-start | bytes 52232 | tf_op jit(solution)/shard_map/ppermute | solution.py:83
  179.3 14.6 %collective-permute-start.29 = (bf16[136,512]{1,0:T(8,128)(2,1)S(1)}, bf16[136,512]{1,0:T(8,128)(2,1)S(1)}, u32[]{:S(2)}, u32[]{:S(2)}) collective-permute-start(bf16[136,512]{1,0:T(8,128)(2,1)S(1)} %dynamic_update_slice.55), channel_id=1, source_target_pairs={{0,128},{4,132},{8,136},{12,140},{16,144},{20,148},{24,152},{28,15... | collective-permute-start | bytes 417800 | tf_op jit(solution)/shard_map/ppermute | solution.py:83
  182.0 21.6 %collective-permute-start.35 = (bf16[136,512]{1,0:T(8,128)(2,1)S(1)}, bf16[136,512]{1,0:T(8,128)(2,1)S(1)}, u32[]{:S(2)}, u32[]{:S(2)}) collective-permute-start(bf16[136,512]{1,0:T(8,128)(2,1)S(1)} %dynamic_update_slice.55), channel_id=1, source_target_pairs={{0,140},{4,136},{8,132},{12,128},{16,156},{20,152},{24,148},{28,14... | collective-permute-start | bytes 417800 | tf_op jit(solution)/shard_map/ppermute | solution.py:83
  188.2 15.2 %collective-permute-start.34 = (bf16[136,512]{1,0:T(8,128)(2,1)S(1)}, bf16[136,512]{1,0:T(8,128)(2,1)S(1)}, u32[]{:S(2)}, u32[]{:S(2)}) collective-permute-start(bf16[136,512]{1,0:T(8,128)(2,1)S(1)} %dynamic_update_slice.55), channel_id=1, source_target_pairs={{0,12},{4,8},{8,4},{12,0},{16,28},{20,24},{24,20},{28,16},{32,44},... | collective-permute-start | bytes 417800 | tf_op jit(solution)/shard_map/ppermute | solution.py:83
  188.2 15.2 %collective-permute-start.33 = (bf16[136,512]{1,0:T(8,128)(2,1)S(1)}, bf16[136,512]{1,0:T(8,128)(2,1)S(1)}, u32[]{:S(2)}, u32[]{:S(2)}) collective-permute-start(bf16[136,512]{1,0:T(8,128)(2,1)S(1)} %dynamic_update_slice.55), channel_id=1, source_target_pairs={{0,132},{4,128},{8,140},{12,136},{16,148},{20,144},{24,156},{28,15... | collective-permute-start | bytes 417800 | tf_op jit(solution)/shard_map/ppermute | solution.py:83
  188.3 10.1 %collective-permute-start.30 = (bf16[136,512]{1,0:T(8,128)(2,1)S(1)}, bf16[136,512]{1,0:T(8,128)(2,1)S(1)}, u32[]{:S(2)}, u32[]{:S(2)}) collective-permute-start(bf16[136,512]{1,0:T(8,128)(2,1)S(1)} %dynamic_update_slice.55), channel_id=1, source_target_pairs={{0,8},{4,12},{8,0},{12,4},{16,24},{20,28},{24,16},{28,20},{32,40},... | collective-permute-start | bytes 417800 | tf_op jit(solution)/shard_map/ppermute | solution.py:83
  194.0 9.1 %collective-permute-start.31 = (bf16[136,512]{1,0:T(8,128)(2,1)S(1)}, bf16[136,512]{1,0:T(8,128)(2,1)S(1)}, u32[]{:S(2)}, u32[]{:S(2)}) collective-permute-start(bf16[136,512]{1,0:T(8,128)(2,1)S(1)} %dynamic_update_slice.55), channel_id=1, source_target_pairs={{0,136},{4,140},{8,128},{12,132},{16,152},{20,156},{24,144},{28,14... | collective-permute-start | bytes 417800 | tf_op jit(solution)/shard_map/ppermute | solution.py:83
  198.4 5.1 %collective-permute-start.32 = (bf16[136,512]{1,0:T(8,128)(2,1)S(1)}, bf16[136,512]{1,0:T(8,128)(2,1)S(1)}, u32[]{:S(2)}, u32[]{:S(2)}) collective-permute-start(bf16[136,512]{1,0:T(8,128)(2,1)S(1)} %dynamic_update_slice.55), channel_id=1, source_target_pairs={{0,4},{4,0},{8,12},{12,8},{16,20},{20,16},{24,28},{28,24},{32,36},... | collective-permute-start | bytes 417800 | tf_op jit(solution)/shard_map/ppermute | solution.py:83
  (90 other events, 120.3 us)
